TPU v7x, 512 devices: a whole 4x4x16 slice. The times are simulated.
512 devices in a mesh: tile: 64 (over x, y, z_hi, core), exp: 8 (over z_lo).
Axes of the slice: x: 4, y: 4, z: 16 (z_hi: 2, z_lo: 8; z = z_hi * 8 + z_lo), core: 2. Of those that a mesh axis runs over, the one named last changes fastest.
Arguments:
- initial: float32 [3, 16384, 256], P(None, ('exp', 'tile')), parts along dimension 1, may hold values from -6 to 6
- depth_field: float32 [16384, 256], P(('exp', 'tile')), parts along dimension 0, may hold values from 0.5 to 2
- coriolis: float32 [16384, 256], P(('exp', 'tile')), parts along dimension 0, may hold values from -1 to 1
- cell_area: float32 [16384, 256], P(('exp', 'tile')), parts along dimension 0, may hold values from 1 to 2
- face_len: float32 [2, 16384, 256], P(None, ('exp', 'tile')), parts along dimension 1, may hold values from 0.5 to 1
- owners: int32 [32768, 2], P(('exp', 'tile')), parts along dimension 0, may hold values from 0 to 63, as said below
- offsets: int32 [32768, 2], P(('exp', 'tile')), parts along dimension 0, may hold values from 0 to 15
- weights: bfloat16 [32768, 2, 128, 128], P(('exp', 'tile')), parts along dimension 0, may hold values from -0.25 to 0.25
Outputs:
- remapped: float32 [8192, 4, 128], P(('exp', 'tile')), parts along dimension 0
- final_fields: float32 [3, 16384, 256], P(None, ('exp', 'tile')), parts along dimension 1
There are 8 independent parts, one for each index of `exp`. A program takes and returns all parts, laid end to end along the dimension named above; each array names one. Nothing has to cross between parts.
Inputs may be any that keep to these rules, and one draw needn't show every extreme that they name: `owners`: of the 128 intersections of one device's source blocks, at most 4 name the same owner; in every draw one owner is named by exactly 4 intersections of every device.
All inputs are finite; a program needn't handle non-finite values.
Results may differ from a plain program's by a relative error of at most 0.0029.
Values sent between devices are 32-bit elements; how exact they have to be, the bound alone decides.
No kernel may reach another device: no remote copies, remote signals or barrier semaphores. Data moves between devices by JAX's collectives and lax.ppermute only.
A program may use at most 64 MiB of HBM per device.

v0:
```python
import jax
import jax.numpy as jnp
from jax import lax
from jax.sharding import PartitionSpec as P

STEPS = 4
TB = 16


time_step = 0.3


def with_halo(cells, sides, width):
    for axis, dim in sides:
        count = lax.axis_size(axis)
        head = lax.slice_in_dim(cells, 0, width, axis=dim)
        tail = lax.slice_in_dim(cells, cells.shape[dim] - width, cells.shape[dim], axis=dim)
        cells = jnp.concatenate(
            [
                lax.ppermute(tail, axis, [(i, (i + 1) % count) for i in range(count)]),
                cells,
                lax.ppermute(head, axis, [((i + 1) % count, i) for i in range(count)]),
            ],
            axis=dim,
        )
    return cells


def advance(fields, metric):
    height, speed_x, speed_y = (fields[0], fields[1], fields[2])
    depth, rotation, area, east_len, north_len = (
        metric[0],
        metric[1],
        metric[2],
        metric[3],
        metric[4],
    )
    wave_x = jnp.sqrt(jnp.maximum(depth[:-1], depth[1:]))
    edge = east_len[:-1]
    flux_h = edge * (
        0.5 * (depth[:-1] * speed_x[:-1] + depth[1:] * speed_x[1:])
        - 0.5 * wave_x * (height[1:] - height[:-1])
    )
    flux_u = edge * (0.5 * (height[:-1] + height[1:]) - 0.5 * wave_x * (speed_x[1:] - speed_x[:-1]))
    flux_v = edge * (-0.5 * wave_x * (speed_y[1:] - speed_y[:-1]))
    own_h = height[1:-1]
    own_u = speed_x[1:-1]
    own_v = speed_y[1:-1]
    own_d = depth[1:-1]
    own_f = rotation[1:-1]
    own_a = area[1:-1]
    own_n = north_len[1:-1]
    above_h = jnp.concatenate([own_h[:, 1:], own_h[:, -1:]], axis=1)
    above_u = jnp.concatenate([own_u[:, 1:], own_u[:, -1:]], axis=1)
    above_v = jnp.concatenate([own_v[:, 1:], -own_v[:, -1:]], axis=1)
    above_d = jnp.concatenate([own_d[:, 1:], own_d[:, -1:]], axis=1)
    wave_y = jnp.sqrt(jnp.maximum(own_d, above_d))
    north_h = own_n * (0.5 * (own_d * own_v + above_d * above_v) - 0.5 * wave_y * (above_h - own_h))
    north_u = own_n * (-0.5 * wave_y * (above_u - own_u))
    north_v = own_n * (0.5 * (own_h + above_h) - 0.5 * wave_y * (above_v - own_v))
    wall_v = own_n[:, :1] * (own_h[:, :1] - jnp.sqrt(own_d[:, :1]) * own_v[:, :1])
    zeros = jnp.zeros_like(wall_v)
    south_h = jnp.concatenate([zeros, north_h[:, :-1]], axis=1)
    south_u = jnp.concatenate([zeros, north_u[:, :-1]], axis=1)
    south_v = jnp.concatenate([wall_v, north_v[:, :-1]], axis=1)
    factor = time_step / own_a
    new_h = own_h - factor * (flux_h[1:] - flux_h[:-1] + north_h - south_h)
    new_u = (
        own_u - factor * (flux_u[1:] - flux_u[:-1] + north_u - south_u) + time_step * own_f * own_v
    )
    new_v = (
        own_v - factor * (flux_v[1:] - flux_v[:-1] + north_v - south_v) - time_step * own_f * own_u
    )
    return jnp.stack([new_h, new_u, new_v])


def on_device(initial, depth_field, coriolis, cell_area, face_len, owners, offsets, weights):
    metric = jnp.concatenate([jnp.stack([depth_field, coriolis, cell_area]), face_len], axis=0)
    snapshots = []
    metric_ext = with_halo(metric, (("tile", 1),), 1)
    fields = initial
    for number in range(STEPS):
        fields = advance(with_halo(fields, (("tile", 1),), 1), metric_ext)
        snapshots.append(fields[0])
    snapped = jnp.stack(snapshots).astype(jnp.bfloat16).reshape(STEPS, -1, 128)
    contribution = jnp.einsum(
        "sbk,brkt->brst", snapped, weights, preferred_element_type=jnp.float32
    )
    slot_count = weights.shape[0] * weights.shape[1]
    flat = contribution.reshape(slot_count, STEPS * 128)
    owner_list = owners.reshape(-1)
    offset_list = offsets.reshape(-1)
    target = owner_list * TB + offset_list
    rows_here = jnp.arange(TB * lax.axis_size("tile"), dtype=jnp.int32)
    select = (rows_here[:, None] == target[None, :]).astype(jnp.float32)
    gathered = lax.psum_scatter(
        jnp.dot(select, flat, precision=lax.Precision.HIGHEST, preferred_element_type=jnp.float32),
        "tile",
        scatter_dimension=0,
        tiled=True,
    )
    return (gathered.reshape(TB, STEPS, 128), fields)


def solution(mesh):
    placed = (
        P(None, ("exp", "tile"), None),
        P(("exp", "tile"), None),
        P(("exp", "tile"), None),
        P(("exp", "tile"), None),
        P(None, ("exp", "tile"), None),
        P(("exp", "tile"), None),
        P(("exp", "tile"), None),
        P(("exp", "tile"), None, None, None),
    )
    return jax.shard_map(
        on_device,
        mesh=mesh,
        in_specs=placed,
        out_specs=(P(("exp", "tile"), None, None), P(None, ("exp", "tile"), None)),
        check_vma=False,
    )
```

profile of v0, /device:TPU:32, one launch (start us, length us, event | category | flops | bytes accessed | tf_op | source)
XLA Modules:
  0.0 703.7 jit_solution(8489532657507430480)
XLA Ops:
  8.0 1.9 collective-permute-start.1
  9.9 18.9 %collective-permute-start.3 = (f32[3,1,256]{2,1,0:T(1,128)S(1)}, f32[3,1,256]{2,1,0:T(1,128)S(1)}, u32[]{:S(2)}, u32[]{:S(2)}) collective-permute-start(f32[3,1,256]{2,1,0:T(1,128)S(1)} %get-tuple-element.59), channel_id=1, source_target_pairs={{8,0},{16,8},{24,16},{32,24},{40,32},{48,40},{56,48},{64,56},{72,6... | collective-permute-start | bytes 9224 | tf_op jit(solution)/shard_map/ppermute | solution.py:22
  29.7 2.6 collective-permute-start.2
  32.3 1.9 collective-permute-start
  38.4 0.9 fusion.93
  39.3 0.9 subtract_multiply_fusion.14
  40.2 0.9 constant_dynamic-update-slice_fusion
  41.5 8.7 %collective-permute-done = f32[5,1,256]{2,1,0:T(1,128)S(1)} collective-permute-done((f32[5,1,256]{2,1,0:T(1,128)S(1)}, f32[5,1,256]{2,1,0:T(1,128)S(1)}, u32[]{:S(2)}, u32[]{:S(2)}) %collective-permute-start) | collective-permute-done | bytes 5152 | tf_op jit(solution)/shard_map/ppermute | solution.py:20
  50.1 0.9 subtract_multiply_fusion.6
  51.9 0.9 fusion.86
  54.8 7.9 %collective-permute-start.5 = (f32[3,1,256]{2,1,0:T(1,128)S(1)}, f32[3,1,256]{2,1,0:T(1,128)S(1)}, u32[]{:S(2)}, u32[]{:S(2)}) collective-permute-start(f32[3,1,256]{2,1,0:T(1,128)S(1)} %get-tuple-element.56), channel_id=1, source_target_pairs={{8,0},{16,8},{24,16},{32,24},{40,32},{48,40},{56,48},{64,56},{72,6... | collective-permute-start | bytes 9224 | tf_op jit(solution)/shard_map/ppermute | solution.py:22
  62.7 1.9 collective-permute-start.4
  64.6 0.9 subtract_multiply_fusion.12
  65.6 14.9 %collective-permute-done.4 = f32[3,1,256]{2,1,0:T(1,128)S(1)} collective-permute-done((f32[3,1,256]{2,1,0:T(1,128)S(1)}, f32[3,1,256]{2,1,0:T(1,128)S(1)}, u32[]{:S(2)}, u32[]{:S(2)}) %collective-permute-start.4) | collective-permute-done | bytes 3104 | tf_op jit(solution)/shard_map/ppermute | solution.py:20
  81.1 1.9 collective-permute-start.7
  83.1 2.4 collective-permute-start.6
  85.7 15.2 %collective-permute-done.6 = f32[3,1,256]{2,1,0:T(1,128)S(1)} collective-permute-done((f32[3,1,256]{2,1,0:T(1,128)S(1)}, f32[3,1,256]{2,1,0:T(1,128)S(1)}, u32[]{:S(2)}, u32[]{:S(2)}) %collective-permute-start.6) | collective-permute-done | bytes 3104 | tf_op jit(solution)/shard_map/ppermute | solution.py:20
  101.5 1.9 collective-permute-start.9
  103.4 2.4 collective-permute-start.8
  106.0 15.2 %collective-permute-done.8 = f32[3,1,256]{2,1,0:T(1,128)S(1)} collective-permute-done((f32[3,1,256]{2,1,0:T(1,128)S(1)}, f32[3,1,256]{2,1,0:T(1,128)S(1)}, u32[]{:S(2)}, u32[]{:S(2)}) %collective-permute-start.8) | collective-permute-done | bytes 3104 | tf_op jit(solution)/shard_map/ppermute | solution.py:20
  121.5 2.9 fusion.4
  124.3 2.4 fusion
  127.4 568.1 %reduce-scatter.2.cloned.1.call-done = f32[16,512]{1,0:T(8,128)} async-done(((f32[1024,512]{1,0:T(8,128)}), f32[16,512]{1,0:T(8,128)}) %reduce-scatter.2.cloned.1.call-update) | async-done | bytes 32784 | tf_op jit(solution)/shard_map/reduce_scatter | solution.py:96
  695.5 1.4 reshape.156
  (69 shorter events, 11.4 us)
Async XLA Ops:
  7.2 58.3 %copy-start.1 = (f32[2,32,256]{2,1,0:T(8,128)S(1)}, f32[2,32,256]{2,1,0:T(8,128)}, u32[]{:S(2)}) copy-start(f32[2,32,256]{2,1,0:T(8,128)} %param.12) | copy-start | bytes 196612
  7.2 73.4 %copy-start.3 = (f32[32,256]{1,0:T(8,128)S(1)}, f32[32,256]{1,0:T(8,128)}, u32[]{:S(2)}) copy-start(f32[32,256]{1,0:T(8,128)} %param.10) | copy-start | bytes 98308
  7.2 73.4 %copy-start.2 = (f32[32,256]{1,0:T(8,128)S(1)}, f32[32,256]{1,0:T(8,128)}, u32[]{:S(2)}) copy-start(f32[32,256]{1,0:T(8,128)} %param.11) | copy-start | bytes 98308
  7.2 73.8 %copy-start = (f32[32,256]{1,0:T(8,128)S(1)}, f32[32,256]{1,0:T(8,128)}, u32[]{:S(2)}) copy-start(f32[32,256]{1,0:T(8,128)} %param.9) | copy-start | bytes 98308
  7.2 688.3 %reduce-scatter.2.cloned.1.call-start = ((), (), s32[]{:S(2)}) async-start(), calls=%async_computation.1 | async-start | bytes 2129920 | tf_op jit(solution)/shard_map/reduce_scatter | solution.py:96
  8.0 33.4 %collective-permute-start.1 = (f32[3,1,256]{2,1,0:T(1,128)S(1)}, f32[3,1,256]{2,1,0:T(1,128)S(1)}, u32[]{:S(2)}, u32[]{:S(2)}) collective-permute-start(f32[3,1,256]{2,1,0:T(1,128)S(1)} %get-tuple-element.58), channel_id=1, source_target_pairs={{0,8},{8,16},{16,24},{24,32},{32,40},{40,48},{48,56},{56,64},{64,7... | collective-permute-start | bytes 9224 | tf_op jit(solution)/shard_map/ppermute | solution.py:20
  9.9 31.4 %collective-permute-start.3 = (f32[3,1,256]{2,1,0:T(1,128)S(1)}, f32[3,1,256]{2,1,0:T(1,128)S(1)}, u32[]{:S(2)}, u32[]{:S(2)}) collective-permute-start(f32[3,1,256]{2,1,0:T(1,128)S(1)} %get-tuple-element.59), channel_id=1, source_target_pairs={{8,0},{16,8},{24,16},{32,24},{40,32},{48,40},{56,48},{64,56},{72,6... | collective-permute-start | bytes 9224 | tf_op jit(solution)/shard_map/ppermute | solution.py:22
  29.7 11.8 %collective-permute-start.2 = (f32[5,1,256]{2,1,0:T(1,128)S(1)}, f32[5,1,256]{2,1,0:T(1,128)S(1)}, u32[]{:S(2)}, u32[]{:S(2)}) collective-permute-start(f32[5,1,256]{2,1,0:T(1,128)S(1)} %get-tuple-element.38), channel_id=1, source_target_pairs={{8,0},{16,8},{24,16},{32,24},{40,32},{48,40},{56,48},{64,56},{72,6... | collective-permute-start | bytes 15368 | tf_op jit(solution)/shard_map/ppermute | solution.py:22
  32.3 17.9 %collective-permute-start = (f32[5,1,256]{2,1,0:T(1,128)S(1)}, f32[5,1,256]{2,1,0:T(1,128)S(1)}, u32[]{:S(2)}, u32[]{:S(2)}) collective-permute-start(f32[5,1,256]{2,1,0:T(1,128)S(1)} %get-tuple-element.39), channel_id=1, source_target_pairs={{0,8},{8,16},{16,24},{24,32},{32,40},{40,48},{48,56},{56,64},{64,7... | collective-permute-start | bytes 15368 | tf_op jit(solution)/shard_map/ppermute | solution.py:20
  54.8 10.8 %collective-permute-start.5 = (f32[3,1,256]{2,1,0:T(1,128)S(1)}, f32[3,1,256]{2,1,0:T(1,128)S(1)}, u32[]{:S(2)}, u32[]{:S(2)}) collective-permute-start(f32[3,1,256]{2,1,0:T(1,128)S(1)} %get-tuple-element.56), channel_id=1, source_target_pairs={{8,0},{16,8},{24,16},{32,24},{40,32},{48,40},{56,48},{64,56},{72,6... | collective-permute-start | bytes 9224 | tf_op jit(solution)/shard_map/ppermute | solution.py:22
  62.7 17.8 %collective-permute-start.4 = (f32[3,1,256]{2,1,0:T(1,128)S(1)}, f32[3,1,256]{2,1,0:T(1,128)S(1)}, u32[]{:S(2)}, u32[]{:S(2)}) collective-permute-start(f32[3,1,256]{2,1,0:T(1,128)S(1)} %get-tuple-element.57), channel_id=1, source_target_pairs={{0,8},{8,16},{16,24},{24,32},{32,40},{40,48},{48,56},{56,64},{64,7... | collective-permute-start | bytes 9224 | tf_op jit(solution)/shard_map/ppermute | solution.py:20
  81.1 4.5 collective-permute-start.7
  83.1 17.8 %collective-permute-start.6 = (f32[3,1,256]{2,1,0:T(1,128)S(1)}, f32[3,1,256]{2,1,0:T(1,128)S(1)}, u32[]{:S(2)}, u32[]{:S(2)}) collective-permute-start(f32[3,1,256]{2,1,0:T(1,128)S(1)} %get-tuple-element.53), channel_id=1, source_target_pairs={{0,8},{8,16},{16,24},{24,32},{32,40},{40,48},{48,56},{56,64},{64,7... | collective-permute-start | bytes 9224 | tf_op jit(solution)/shard_map/ppermute | solution.py:20
  101.5 4.5 collective-permute-start.9
  103.4 17.8 %collective-permute-start.8 = (f32[3,1,256]{2,1,0:T(1,128)S(1)}, f32[3,1,256]{2,1,0:T(1,128)S(1)}, u32[]{:S(2)}, u32[]{:S(2)}) collective-permute-start(f32[3,1,256]{2,1,0:T(1,128)S(1)} %get-tuple-element.49), channel_id=1, source_target_pairs={{0,8},{8,16},{16,24},{24,32},{32,40},{40,48},{48,56},{56,64},{64,7... | collective-permute-start | bytes 9224 | tf_op jit(solution)/shard_map/ppermute | solution.py:20
Sparse Core Ops, SparseCore 0:
  126.8 568.6 reduce-scatter.1
where the time goes:
time: 705 us; the launch traced here: 704 us
  waiting for transfers between devices  622 us (88%)
  starting transfers between devices  43.8 us (6%)
  between operations  14.3 us (2%)
  other arithmetic  11.1 us (2%)
    reduce_scatter x1, waiting for transfers between devices, on_device(): lax.psum_scatter(jnp.dot(select, flat, precision=lax.Precision.HIGHEST, p...  568 us
    ppermute x5, waiting for transfers between devices, with_halo(): lax.ppermute(tail, axis, [(i, (i + 1) % count) for i in range(count)])  54.1 us
    ppermute x5, starting transfers between devices, with_halo(): lax.ppermute(head, axis, [((i + 1) % count, i) for i in range(count)])  33.2 us
  transfers between devices with their start and end apart: 11, of which 5 were waited for; matrix products, arithmetic and copies ran while one was open for 1% of the time, Pallas kernels for 0%

commit v1 on v0

--- a/solution.py
+++ b/solution.py
@@ -5,6 +5,7 @@
 
 STEPS = 4
 TB = 16
+CAP = 4
 
 
 time_step = 0.3
@@ -88,16 +89,37 @@
     )
     slot_count = weights.shape[0] * weights.shape[1]
     flat = contribution.reshape(slot_count, STEPS * 128)
-    owner_list = owners.reshape(-1)
-    offset_list = offsets.reshape(-1)
-    target = owner_list * TB + offset_list
-    rows_here = jnp.arange(TB * lax.axis_size("tile"), dtype=jnp.int32)
-    select = (rows_here[:, None] == target[None, :]).astype(jnp.float32)
-    gathered = lax.psum_scatter(
-        jnp.dot(select, flat, precision=lax.Precision.HIGHEST, preferred_element_type=jnp.float32),
-        "tile",
-        scatter_dimension=0,
-        tiled=True,
+    n_tile = lax.axis_size("tile")
+    me = lax.axis_index("tile")
+    labels = jnp.concatenate([owners.reshape(1, -1), offsets.reshape(1, -1)], axis=0)
+    all_labels = lax.all_gather(labels, "tile", axis=0, tiled=False)
+    all_owner = all_labels[:, 0]
+    all_offset = all_labels[:, 1]
+    item = jnp.arange(slot_count, dtype=jnp.int32)
+    earlier = item[None, :] < item[:, None]
+
+    def rank_of(owner_list):
+        same = owner_list[:, None] == owner_list[None, :]
+        return jnp.sum((same & earlier).astype(jnp.int32), axis=1)
+
+    own_owner = owners.reshape(-1)
+    slot = own_owner * CAP + rank_of(own_owner)
+    pack = (jnp.arange(n_tile * CAP, dtype=jnp.int32)[:, None] == slot[None, :]).astype(
+        jnp.float32
+    )
+    send = jnp.dot(pack, flat, precision=lax.Precision.HIGHEST, preferred_element_type=jnp.float32)
+    recv = lax.all_to_all(
+        send.reshape(n_tile, CAP * STEPS * 128), "tile", 0, 0, tiled=True
+    ).reshape(n_tile * CAP, STEPS * 128)
+    ranks = jax.vmap(rank_of)(all_owner)
+    mine = all_owner == me
+    hit_t = (all_offset[:, :, None] == jnp.arange(TB, dtype=jnp.int32)) & mine[:, :, None]
+    hit_r = ranks[:, :, None] == jnp.arange(CAP, dtype=jnp.int32)
+    unpack = jnp.einsum(
+        "djt,djr->tdr", hit_t.astype(jnp.float32), hit_r.astype(jnp.float32)
+    ).reshape(TB, n_tile * CAP)
+    gathered = jnp.dot(
+        unpack, recv, precision=lax.Precision.HIGHEST, preferred_element_type=jnp.float32
     )
     return (gathered.reshape(TB, STEPS, 128), fields)
 

time: 705 us -> 307 us (0.44)
  waiting for transfers between devices: 622 us -> 11 us
  blocking collectives: 0 us -> 167 us
  starting transfers between devices: 43.8 us -> 97.7 us
  between operations: 14.3 us -> 1.01 us
    reduce_scatter x1 -> x0, waiting for transfers between devices: 568 us -> none  [on_device(): lax.psum_scatter(jnp.dot(select, flat, precision=lax.Precision.HIGHEST, p...]
    all_gather x0 -> x1, blocking collectives: none -> 167 us  [on_device(): all_labels = lax.all_gather(labels, 'tile', axis=0, tiled=False)]
    ppermute x5, waiting for transfers between devices: 54.1 us -> 8.53 us  [with_halo(): lax.ppermute(tail, axis, [(i, (i + 1) % count) for i in range(count)])]
    ppermute x5, starting transfers between devices: 33.2 us -> 71.2 us  [with_halo(): lax.ppermute(head, axis, [((i + 1) % count, i) for i in range(count)])]
    all_to_all x0 -> x1, starting transfers between devices: none -> 16.9 us  [on_device(): lax.all_to_all(send.reshape(n_tile, CAP * STEPS * 128), 'tile', 0, 0, til...]
  transfers between devices with their start and end apart: 11 -> 11, of which waited for: 5 -> 4; matrix products, arithmetic and copies ran while one was open for 1% -> 4% of each run, Pallas kernels for 0% -> 0%
where the time goes in v1:
time: 307 us; the launch traced here: 305 us
  blocking collectives  167 us (54%)
  starting transfers between devices  97.7 us (32%)
  other arithmetic  14.4 us (5%)
  waiting for transfers between devices  11 us (4%)
  local copies, waits for them, and re-layouts  9.1 us (3%)
  matrix products  4.08 us (1%)
    all_gather x1, blocking collectives, on_device(): all_labels = lax.all_gather(labels, 'tile', axis=0, tiled=False)  167 us
    ppermute x5, starting transfers between devices, with_halo(): lax.ppermute(head, axis, [((i + 1) % count, i) for i in range(count)])  71.2 us
    all_to_all x1, starting transfers between devices, on_device(): lax.all_to_all(send.reshape(n_tile, CAP * STEPS * 128), 'tile', 0, 0, til...  16.9 us
    ppermute x5, starting transfers between devices, with_halo(): lax.ppermute(tail, axis, [(i, (i + 1) % count) for i in range(count)])  9.61 us
    ppermute x5, waiting for transfers between devices, with_halo(): lax.ppermute(tail, axis, [(i, (i + 1) % count) for i in range(count)])  8.53 us
  transfers between devices with their start and end apart: 11, of which 4 were waited for; matrix products, arithmetic and copies ran while one was open for 4% of the time, Pallas kernels for 0%

profile of v1, /device:TPU:32, one launch (start us, length us, event | category | flops | bytes accessed | tf_op | source)
XLA Modules:
  0.0 304.8 jit_solution(3586654422629545544)
XLA Ops:
  1.5 1.9 collective-permute-start
  3.5 18.9 %collective-permute-start.2 = (f32[5,1,256]{2,1,0:T(1,128)S(1)}, f32[5,1,256]{2,1,0:T(1,128)S(1)}, u32[]{:S(2)}, u32[]{:S(2)}) collective-permute-start(f32[5,1,256]{2,1,0:T(1,128)S(1)} %get-tuple-element.46), channel_id=1, source_target_pairs={{8,0},{16,8},{24,16},{32,24},{40,32},{48,40},{56,48},{64,56},{72,6... | collective-permute-start | bytes 15368 | tf_op jit(solution)/shard_map/ppermute | solution.py:23
  23.1 2.6 collective-permute-start.3
  25.7 1.9 collective-permute-start.1
  32.3 0.9 fusion.99
  33.2 0.9 subtract_multiply_fusion.14
  34.1 0.9 constant_dynamic-update-slice_fusion
  35.1 8.5 %collective-permute-done.1 = f32[3,1,256]{2,1,0:T(1,128)S(1)} collective-permute-done((f32[3,1,256]{2,1,0:T(1,128)S(1)}, f32[3,1,256]{2,1,0:T(1,128)S(1)}, u32[]{:S(2)}, u32[]{:S(2)}) %collective-permute-start.1) | collective-permute-done | bytes 3104 | tf_op jit(solution)/shard_map/ppermute | solution.py:21
  43.6 0.9 subtract_multiply_fusion.6
  46.3 0.9 fusion.92
  48.2 1.9 collective-permute-start.4
  50.1 16.6 %collective-permute-start.5 = (f32[3,1,256]{2,1,0:T(1,128)S(1)}, f32[3,1,256]{2,1,0:T(1,128)S(1)}, u32[]{:S(2)}, u32[]{:S(2)}) collective-permute-start(f32[3,1,256]{2,1,0:T(1,128)S(1)} %get-tuple-element.64), channel_id=1, source_target_pairs={{8,0},{16,8},{24,16},{32,24},{40,32},{48,40},{56,48},{64,56},{72,6... | collective-permute-start | bytes 9224 | tf_op jit(solution)/shard_map/ppermute | solution.py:23
  68.6 1.9 collective-permute-start.6
  70.5 16.6 %collective-permute-start.7 = (f32[3,1,256]{2,1,0:T(1,128)S(1)}, f32[3,1,256]{2,1,0:T(1,128)S(1)}, u32[]{:S(2)}, u32[]{:S(2)}) collective-permute-start(f32[3,1,256]{2,1,0:T(1,128)S(1)} %get-tuple-element.60), channel_id=1, source_target_pairs={{8,0},{16,8},{24,16},{32,24},{40,32},{48,40},{56,48},{64,56},{72,6... | collective-permute-start | bytes 9224 | tf_op jit(solution)/shard_map/ppermute | solution.py:23
  87.3 1.1 collective-permute-done.7
  89.0 1.9 collective-permute-start.8
  90.9 16.6 %collective-permute-start.9 = (f32[3,1,256]{2,1,0:T(1,128)S(1)}, f32[3,1,256]{2,1,0:T(1,128)S(1)}, u32[]{:S(2)}, u32[]{:S(2)}) collective-permute-start(f32[3,1,256]{2,1,0:T(1,128)S(1)} %get-tuple-element.56), channel_id=1, source_target_pairs={{8,0},{16,8},{24,16},{32,24},{40,32},{48,40},{56,48},{64,56},{72,6... | collective-permute-start | bytes 9224 | tf_op jit(solution)/shard_map/ppermute | solution.py:23
  107.7 1.1 collective-permute-done.9
  109.0 2.9 fusion.8
  112.2 1.4 all_to_all.8
  113.7 16.9 %all-to-all-start = ((f32[64,1,2048]{2,1,0:T(1,128)}), f32[64,1,2048]{2,1,0:T(1,128)S(1)}, u32[]{:S(2)}, u32[]{:S(2)}) async-start(f32[64,1,2048]{2,1,0:T(1,128)} %all_to_all.8), calls=%async_computation | async-start | bytes 1048576 | tf_op jit(solution)/shard_map/all_to_all | solution.py:111
  131.0 167.4 %all-gather.1 = s32[64,2,128]{2,1,0:T(2,128)S(1)} all-gather(s32[1,2,128]{2,1,0:T(2,128)S(1)} %add_bitcast_fusion), channel_id=2, replica_groups=mesh['tile'=64,'exp'=8] {'tile'}, dimensions={0}, use_global_device_ids=true | all-gather | bytes 66560 | tf_op jit(solution)/shard_map/all_gather | solution.py:95
  298.4 2.6 convert_reduce_fusion
  301.9 1.2 reduce
  (86 shorter events, 15.4 us)
Async XLA Ops:
  0.6 67.6 %copy-start = (f32[32,256]{1,0:T(8,128)S(1)}, f32[32,256]{1,0:T(8,128)}, u32[]{:S(2)}) copy-start(f32[32,256]{1,0:T(8,128)} %param.9) | copy-start | bytes 98308
  0.6 67.4 %copy-start.3 = (f32[32,256]{1,0:T(8,128)S(1)}, f32[32,256]{1,0:T(8,128)}, u32[]{:S(2)}) copy-start(f32[32,256]{1,0:T(8,128)} %param.10) | copy-start | bytes 98308
  0.7 67.4 %copy-start.2 = (f32[32,256]{1,0:T(8,128)S(1)}, f32[32,256]{1,0:T(8,128)}, u32[]{:S(2)}) copy-start(f32[32,256]{1,0:T(8,128)} %param.11) | copy-start | bytes 98308
  0.7 66.9 %copy-start.1 = (f32[2,32,256]{2,1,0:T(8,128)S(1)}, f32[2,32,256]{2,1,0:T(8,128)}, u32[]{:S(2)}) copy-start(f32[2,32,256]{2,1,0:T(8,128)} %param.12) | copy-start | bytes 196612
  1.5 42.0 %collective-permute-start = (f32[5,1,256]{2,1,0:T(1,128)S(1)}, f32[5,1,256]{2,1,0:T(1,128)S(1)}, u32[]{:S(2)}, u32[]{:S(2)}) collective-permute-start(f32[5,1,256]{2,1,0:T(1,128)S(1)} %get-tuple-element.47), channel_id=1, source_target_pairs={{0,8},{8,16},{16,24},{24,32},{32,40},{40,48},{48,56},{56,64},{64,7... | collective-permute-start | bytes 15368 | tf_op jit(solution)/shard_map/ppermute | solution.py:21
  3.5 40.1 %collective-permute-start.2 = (f32[5,1,256]{2,1,0:T(1,128)S(1)}, f32[5,1,256]{2,1,0:T(1,128)S(1)}, u32[]{:S(2)}, u32[]{:S(2)}) collective-permute-start(f32[5,1,256]{2,1,0:T(1,128)S(1)} %get-tuple-element.46), channel_id=1, source_target_pairs={{8,0},{16,8},{24,16},{32,24},{40,32},{48,40},{56,48},{64,56},{72,6... | collective-permute-start | bytes 15368 | tf_op jit(solution)/shard_map/ppermute | solution.py:23
  23.1 11.8 %collective-permute-start.3 = (f32[3,1,256]{2,1,0:T(1,128)S(1)}, f32[3,1,256]{2,1,0:T(1,128)S(1)}, u32[]{:S(2)}, u32[]{:S(2)}) collective-permute-start(f32[3,1,256]{2,1,0:T(1,128)S(1)} %get-tuple-element.67), channel_id=1, source_target_pairs={{8,0},{16,8},{24,16},{32,24},{40,32},{48,40},{56,48},{64,56},{72,6... | collective-permute-start | bytes 9224 | tf_op jit(solution)/shard_map/ppermute | solution.py:23
  25.7 17.8 %collective-permute-start.1 = (f32[3,1,256]{2,1,0:T(1,128)S(1)}, f32[3,1,256]{2,1,0:T(1,128)S(1)}, u32[]{:S(2)}, u32[]{:S(2)}) collective-permute-start(f32[3,1,256]{2,1,0:T(1,128)S(1)} %get-tuple-element.66), channel_id=1, source_target_pairs={{0,8},{8,16},{16,24},{24,32},{32,40},{40,48},{48,56},{56,64},{64,7... | collective-permute-start | bytes 9224 | tf_op jit(solution)/shard_map/ppermute | solution.py:21
  48.2 19.5 %collective-permute-start.4 = (f32[3,1,256]{2,1,0:T(1,128)S(1)}, f32[3,1,256]{2,1,0:T(1,128)S(1)}, u32[]{:S(2)}, u32[]{:S(2)}) collective-permute-start(f32[3,1,256]{2,1,0:T(1,128)S(1)} %get-tuple-element.65), channel_id=1, source_target_pairs={{0,8},{8,16},{16,24},{24,32},{32,40},{40,48},{48,56},{56,64},{64,7... | collective-permute-start | bytes 9224 | tf_op jit(solution)/shard_map/ppermute | solution.py:21
  50.1 17.9 %collective-permute-start.5 = (f32[3,1,256]{2,1,0:T(1,128)S(1)}, f32[3,1,256]{2,1,0:T(1,128)S(1)}, u32[]{:S(2)}, u32[]{:S(2)}) collective-permute-start(f32[3,1,256]{2,1,0:T(1,128)S(1)} %get-tuple-element.64), channel_id=1, source_target_pairs={{8,0},{16,8},{24,16},{32,24},{40,32},{48,40},{56,48},{64,56},{72,6... | collective-permute-start | bytes 9224 | tf_op jit(solution)/shard_map/ppermute | solution.py:23
  68.6 18.7 %collective-permute-start.6 = (f32[3,1,256]{2,1,0:T(1,128)S(1)}, f32[3,1,256]{2,1,0:T(1,128)S(1)}, u32[]{:S(2)}, u32[]{:S(2)}) collective-permute-start(f32[3,1,256]{2,1,0:T(1,128)S(1)} %get-tuple-element.61), channel_id=1, source_target_pairs={{0,8},{8,16},{16,24},{24,32},{32,40},{40,48},{48,56},{56,64},{64,7... | collective-permute-start | bytes 9224 | tf_op jit(solution)/shard_map/ppermute | solution.py:21
  70.5 17.9 %collective-permute-start.7 = (f32[3,1,256]{2,1,0:T(1,128)S(1)}, f32[3,1,256]{2,1,0:T(1,128)S(1)}, u32[]{:S(2)}, u32[]{:S(2)}) collective-permute-start(f32[3,1,256]{2,1,0:T(1,128)S(1)} %get-tuple-element.60), channel_id=1, source_target_pairs={{8,0},{16,8},{24,16},{32,24},{40,32},{48,40},{56,48},{64,56},{72,6... | collective-permute-start | bytes 9224 | tf_op jit(solution)/shard_map/ppermute | solution.py:23
  89.0 18.7 %collective-permute-start.8 = (f32[3,1,256]{2,1,0:T(1,128)S(1)}, f32[3,1,256]{2,1,0:T(1,128)S(1)}, u32[]{:S(2)}, u32[]{:S(2)}) collective-permute-start(f32[3,1,256]{2,1,0:T(1,128)S(1)} %get-tuple-element.57), channel_id=1, source_target_pairs={{0,8},{8,16},{16,24},{24,32},{32,40},{40,48},{48,56},{56,64},{64,7... | collective-permute-start | bytes 9224 | tf_op jit(solution)/shard_map/ppermute | solution.py:21
  90.9 17.9 %collective-permute-start.9 = (f32[3,1,256]{2,1,0:T(1,128)S(1)}, f32[3,1,256]{2,1,0:T(1,128)S(1)}, u32[]{:S(2)}, u32[]{:S(2)}) collective-permute-start(f32[3,1,256]{2,1,0:T(1,128)S(1)} %get-tuple-element.56), channel_id=1, source_target_pairs={{8,0},{16,8},{24,16},{32,24},{40,32},{48,40},{56,48},{64,56},{72,6... | collective-permute-start | bytes 9224 | tf_op jit(solution)/shard_map/ppermute | solution.py:23
  108.8 21.9 %copy-start.4 = (s32[64,2]{0,1:T(2,128)S(1)}, s32[64,2]{0,1:T(2,128)}, u32[]{:S(2)}) copy-start(s32[64,2]{0,1:T(2,128)} %param.14) | copy-start | bytes 1540
  113.7 188.3 %all-to-all-start = ((f32[64,1,2048]{2,1,0:T(1,128)}), f32[64,1,2048]{2,1,0:T(1,128)S(1)}, u32[]{:S(2)}, u32[]{:S(2)}) async-start(f32[64,1,2048]{2,1,0:T(1,128)} %all_to_all.8), calls=%async_computation | async-start | bytes 1048576 | tf_op jit(solution)/shard_map/all_to_all | solution.py:111

commit v2 on v0

--- a/solution.py
+++ b/solution.py
@@ -5,6 +5,7 @@
 
 STEPS = 4
 TB = 16
+CAP = 4
 
 
 time_step = 0.3
@@ -75,29 +76,50 @@
 
 
 def on_device(initial, depth_field, coriolis, cell_area, face_len, owners, offsets, weights):
-    metric = jnp.concatenate([jnp.stack([depth_field, coriolis, cell_area]), face_len], axis=0)
+    cells = jnp.concatenate(
+        [initial, jnp.stack([depth_field, coriolis, cell_area]), face_len], axis=0
+    )
+    cells_ext = with_halo(cells, (("tile", 1),), STEPS)
+    width = cells_ext.shape[1]
+    fields = cells_ext[:3]
     snapshots = []
-    metric_ext = with_halo(metric, (("tile", 1),), 1)
-    fields = initial
     for number in range(STEPS):
-        fields = advance(with_halo(fields, (("tile", 1),), 1), metric_ext)
-        snapshots.append(fields[0])
+        metric_ext = cells_ext[3:, number : width - number]
+        fields = advance(fields, metric_ext)
+        keep = STEPS - 1 - number
+        snapshots.append(fields[0, keep : fields.shape[1] - keep])
     snapped = jnp.stack(snapshots).astype(jnp.bfloat16).reshape(STEPS, -1, 128)
     contribution = jnp.einsum(
         "sbk,brkt->brst", snapped, weights, preferred_element_type=jnp.float32
     )
     slot_count = weights.shape[0] * weights.shape[1]
     flat = contribution.reshape(slot_count, STEPS * 128)
-    owner_list = owners.reshape(-1)
-    offset_list = offsets.reshape(-1)
-    target = owner_list * TB + offset_list
-    rows_here = jnp.arange(TB * lax.axis_size("tile"), dtype=jnp.int32)
-    select = (rows_here[:, None] == target[None, :]).astype(jnp.float32)
-    gathered = lax.psum_scatter(
-        jnp.dot(select, flat, precision=lax.Precision.HIGHEST, preferred_element_type=jnp.float32),
-        "tile",
-        scatter_dimension=0,
-        tiled=True,
+    n_tile = lax.axis_size("tile")
+    item = jnp.arange(slot_count, dtype=jnp.int32)
+    own_owner = owners.reshape(-1)
+    same = own_owner[:, None] == own_owner[None, :]
+    rank = jnp.sum((same & (item[None, :] < item[:, None])).astype(jnp.int32), axis=1)
+    slot = own_owner * CAP + rank
+    pack = (jnp.arange(n_tile * CAP, dtype=jnp.int32)[:, None] == slot[None, :]).astype(
+        jnp.float32
+    )
+    send = jnp.dot(pack, flat, precision=lax.Precision.HIGHEST, preferred_element_type=jnp.float32)
+    labels = jnp.dot(
+        pack,
+        offsets.reshape(-1, 1).astype(jnp.float32) + 1.0,
+        precision=lax.Precision.HIGHEST,
+        preferred_element_type=jnp.float32,
+    ).reshape(n_tile, CAP) - 1.0
+    label_row = jnp.pad(labels, ((0, 0), (0, 128 - CAP)))
+    payload = jnp.concatenate([send.reshape(n_tile, CAP * STEPS * 128), label_row], axis=1)
+    recv = lax.all_to_all(payload, "tile", 0, 0, tiled=True)
+    recv_data = recv[:, : CAP * STEPS * 128].reshape(n_tile * CAP, STEPS * 128)
+    recv_offset = recv[:, CAP * STEPS * 128 : CAP * STEPS * 128 + CAP].reshape(-1)
+    unpack = (
+        recv_offset[None, :] == jnp.arange(TB, dtype=jnp.float32)[:, None]
+    ).astype(jnp.float32)
+    gathered = jnp.dot(
+        unpack, recv_data, precision=lax.Precision.HIGHEST, preferred_element_type=jnp.float32
     )
     return (gathered.reshape(TB, STEPS, 128), fields)
 

time: 705 us -> 94.2 us (0.13)
  waiting for transfers between devices: 622 us -> 38.3 us
  between operations: 14.3 us -> 0.99 us
  starting transfers between devices: 43.8 us -> 35.2 us
  other arithmetic: 11.1 us -> 3.84 us
    reduce_scatter x1 -> x0, waiting for transfers between devices: 568 us -> none  [on_device(): lax.psum_scatter(jnp.dot(select, flat, precision=lax.Precision.HIGHEST, p...]
    ppermute x5 -> x1, waiting for transfers between devices: 54.1 us -> 0.01 us  [with_halo(): lax.ppermute(tail, axis, [(i, (i + 1) % count) for i in range(count)])]
    all_to_all x0 -> x1, waiting for transfers between devices: none -> 38.3 us  [on_device(): recv = lax.all_to_all(payload, 'tile', 0, 0, tiled=True)]
    all_to_all x0 -> x1, starting transfers between devices: none -> 14.4 us  [on_device(): recv = lax.all_to_all(payload, 'tile', 0, 0, tiled=True)]
    ppermute x5 -> x1, starting transfers between devices: 33.2 us -> 18.9 us  [with_halo(): lax.ppermute(head, axis, [((i + 1) % count, i) for i in range(count)])]
    ppermute x5 -> x1, starting transfers between devices: 10.6 us -> 1.92 us  [with_halo(): lax.ppermute(tail, axis, [(i, (i + 1) % count) for i in range(count)])]
  transfers between devices with their start and end apart: 11 -> 3, of which waited for: 5 -> 1; matrix products, arithmetic and copies ran while one was open for 1% -> 5% of each run, Pallas kernels for 0% -> 0%
where the time goes in v2:
time: 94.2 us; the launch traced here: 93.3 us
  waiting for transfers between devices  38.3 us (41%)
  starting transfers between devices  35.2 us (37%)
  local copies, waits for them, and re-layouts  11.1 us (12%)
  matrix products  3.86 us (4%)
  other arithmetic  3.84 us (4%)
  between operations  0.99 us (1%)
    all_to_all x1, waiting for transfers between devices, on_device(): recv = lax.all_to_all(payload, 'tile', 0, 0, tiled=True)  38.3 us
    ppermute x1, starting transfers between devices, with_halo(): lax.ppermute(head, axis, [((i + 1) % count, i) for i in range(count)])  18.9 us
    all_to_all x1, starting transfers between devices, on_device(): recv = lax.all_to_all(payload, 'tile', 0, 0, tiled=True)  14.4 us
    unnamed x15, local copies, waits for them, and re-layouts  4.67 us
    dot_general x1, matrix products, on_device(): jnp.einsum('sbk,brkt->brst', snapped, weights, preferred_element_type=jnp...  2.87 us
    ppermute x1, starting transfers between devices, with_halo(): lax.ppermute(tail, axis, [(i, (i + 1) % count) for i in range(count)])  1.92 us
  transfers between devices with their start and end apart: 3, of which 1 were waited for; matrix products, arithmetic and copies ran while one was open for 5% of the time, Pallas kernels for 0%

profile of v2, /device:TPU:32, one launch (start us, length us, event | category | flops | bytes accessed | tf_op | source)
XLA Modules:
  0.0 93.3 jit_solution(14679342415003730009)
XLA Ops:
  0.6 0.9 constant_dynamic-update-slice_fusion.1
  1.5 0.8 bitcast_dynamic-update-slice_fusion.2
  2.3 0.8 bitcast_dynamic-update-slice_fusion.1
  3.1 0.8 bitcast_dynamic-update-slice_fusion
  3.8 0.8 constant_dynamic-update-slice_fusion
  4.7 1.9 %collective-permute-start = (f32[8,4,256]{2,1,0:T(4,128)S(1)}, f32[8,4,256]{2,1,0:T(4,128)S(1)}, u32[]{:S(2)}, u32[]{:S(2)}) collective-permute-start(f32[8,4,256]{2,1,0:T(4,128)S(1)} %get-tuple-element.55), channel_id=1, source_target_pairs={{0,8},{8,16},{16,24},{24,32},{32,40},{40,48},{48,56},{56,64},{64,7... | collective-permute-start | bytes 98312 | tf_op jit(solution)/shard_map/ppermute | solution.py:21
  6.6 18.9 %collective-permute-start.1 = (f32[8,4,256]{2,1,0:T(4,128)S(1)}, f32[8,4,256]{2,1,0:T(4,128)S(1)}, u32[]{:S(2)}, u32[]{:S(2)}) collective-permute-start(f32[8,4,256]{2,1,0:T(4,128)S(1)} %get-tuple-element.56), channel_id=1, source_target_pairs={{8,0},{16,8},{24,16},{32,24},{40,32},{48,40},{56,48},{64,56},{72,6... | collective-permute-start | bytes 98312 | tf_op jit(solution)/shard_map/ppermute | solution.py:23
  25.5 0.8 slice_bitcast_fusion.15
  26.3 0.7 convert_add_fusion
  27.2 0.8 copy.30
  28.1 0.2 convert_reduce_fusion
  28.5 0.3 fusion.3
  28.8 0.8 slice.831
  33.3 2.9 %fusion.5 = f32[64,4,2,128]{3,1,2,0:T(4,128)S(1)} fusion(bf16[64,2,128,128]{3,2,1,0:T(8,128)(2,1)} %param.15, bf16[1,64,128]{2,0,1:T(2,128)(2,1)S(1)} %stack.62, bf16[1,64,128]{2,0,1:T(2,128)(2,1)S(1)} %stack.61, bf16[1,64,128]{2,0,1:T(2,128)(2,1)S(1)} %stack.60, bf16[1,64,128]{2,0,1:T(2,128)(2,1)S(1)} %stack.59), kind=kOutput, calls=%fused_computation.12 | convolution fusion | flops 17039360 | bytes 4521984 | tf_op jit(solution)/shard_map/sbk,brkt->brst/dot_general | solution.py:92
  36.1 0.4 fusion
  36.6 0.2 reshape.144
  36.9 1.2 %all_to_all.8 = f32[64,1,2176]{2,1,0:T(1,128)} reshape(f32[64,2176]{1,0:T(8,128)S(1)} %select_maximum_fusion) | data formatting | bytes 1114112 | tf_op jit(solution)/shard_map/all_to_all | solution.py:115
  38.1 14.4 %all-to-all-start = ((f32[64,1,2176]{2,1,0:T(1,128)}), f32[64,1,2176]{2,1,0:T(1,128)S(1)}, u32[]{:S(2)}, u32[]{:S(2)}) async-start(f32[64,1,2176]{2,1,0:T(1,128)} %all_to_all.8), calls=%async_computation | async-start | bytes 1114112 | tf_op jit(solution)/shard_map/all_to_all | solution.py:115
  52.8 0.6 pad_maximum_fusion.1
  53.4 38.3 %all-to-all-done = f32[64,1,2176]{2,1,0:T(1,128)S(1)} async-done(((f32[64,1,2176]{2,1,0:T(1,128)}), f32[64,1,2176]{2,1,0:T(1,128)S(1)}, u32[]{:S(2)}, u32[]{:S(2)}) %all-to-all-start) | async-done | bytes 557088 | tf_op jit(solution)/shard_map/all_to_all | solution.py:115
  92.0 0.1 reshape.145
  92.1 0.2 copy.36
  92.3 0.3 fusion.108
  92.7 0.7 copy.37
  (78 shorter events, 4.6 us)
Async XLA Ops:
  4.7 25.0 %collective-permute-start = (f32[8,4,256]{2,1,0:T(4,128)S(1)}, f32[8,4,256]{2,1,0:T(4,128)S(1)}, u32[]{:S(2)}, u32[]{:S(2)}) collective-permute-start(f32[8,4,256]{2,1,0:T(4,128)S(1)} %get-tuple-element.55), channel_id=1, source_target_pairs={{0,8},{8,16},{16,24},{24,32},{32,40},{40,48},{48,56},{56,64},{64,7... | collective-permute-start | bytes 98312 | tf_op jit(solution)/shard_map/ppermute | solution.py:21
  6.6 23.1 %collective-permute-start.1 = (f32[8,4,256]{2,1,0:T(4,128)S(1)}, f32[8,4,256]{2,1,0:T(4,128)S(1)}, u32[]{:S(2)}, u32[]{:S(2)}) collective-permute-start(f32[8,4,256]{2,1,0:T(4,128)S(1)} %get-tuple-element.56), channel_id=1, source_target_pairs={{8,0},{16,8},{24,16},{32,24},{40,32},{48,40},{56,48},{64,56},{72,6... | collective-permute-start | bytes 98312 | tf_op jit(solution)/shard_map/ppermute | solution.py:23
  30.2 2.6 %copy-start = (f32[32,256]{1,0:T(8,128)S(1)}, f32[32,256]{1,0:T(8,128)}, u32[]{:S(2)}) copy-start(f32[32,256]{1,0:T(8,128)} %param.9) | copy-start | bytes 98308
  30.6 2.5 %copy-start.1 = (f32[2,32,256]{2,1,0:T(8,128)S(1)}, f32[2,32,256]{2,1,0:T(8,128)}, u32[]{:S(2)}) copy-start(f32[2,32,256]{2,1,0:T(8,128)} %param.12) | copy-start | bytes 196612
  30.7 2.4 %copy-start.2 = (f32[32,256]{1,0:T(8,128)S(1)}, f32[32,256]{1,0:T(8,128)}, u32[]{:S(2)}) copy-start(f32[32,256]{1,0:T(8,128)} %param.11) | copy-start | bytes 98308
  33.3 19.4 %copy-start.3 = (f32[32,256]{1,0:T(8,128)S(1)}, f32[32,256]{1,0:T(8,128)}, u32[]{:S(2)}) copy-start(f32[32,256]{1,0:T(8,128)} %param.10) | copy-start | bytes 98308
  38.1 53.7 %all-to-all-start = ((f32[64,1,2176]{2,1,0:T(1,128)}), f32[64,1,2176]{2,1,0:T(1,128)S(1)}, u32[]{:S(2)}, u32[]{:S(2)}) async-start(f32[64,1,2176]{2,1,0:T(1,128)} %all_to_all.8), calls=%async_computation | async-start | bytes 1114112 | tf_op jit(solution)/shard_map/all_to_all | solution.py:115

commit v3 on v2

--- a/solution.py
+++ b/solution.py
@@ -16,14 +16,22 @@
         count = lax.axis_size(axis)
         head = lax.slice_in_dim(cells, 0, width, axis=dim)
         tail = lax.slice_in_dim(cells, cells.shape[dim] - width, cells.shape[dim], axis=dim)
-        cells = jnp.concatenate(
-            [
-                lax.ppermute(tail, axis, [(i, (i + 1) % count) for i in range(count)]),
-                cells,
-                lax.ppermute(head, axis, [((i + 1) % count, i) for i in range(count)]),
-            ],
-            axis=dim,
-        )
+        if count % 2 == 0:
+            odd = lax.axis_index(axis) % 2 == 1
+            near = lax.ppermute(
+                jnp.where(odd, head, tail), axis, [(i, i ^ 1) for i in range(count)]
+            )
+            far = lax.ppermute(
+                jnp.where(odd, tail, head),
+                axis,
+                [(i, (i + 1) % count if i % 2 else (i - 1) % count) for i in range(count)],
+            )
+            before = jnp.where(odd, near, far)
+            after = jnp.where(odd, far, near)
+        else:
+            before = lax.ppermute(tail, axis, [(i, (i + 1) % count) for i in range(count)])
+            after = lax.ppermute(head, axis, [((i + 1) % count, i) for i in range(count)])
+        cells = jnp.concatenate([before, cells, after], axis=dim)
     return cells
 
 

time: 94.2 us -> 95.3 us (1.012)
  no operation moved by 1% of the time
where the time goes in v3:
time: 95.3 us; the launch traced here: 94.4 us
  waiting for transfers between devices  38.8 us (41%)
  starting transfers between devices  35.8 us (38%)
  local copies, waits for them, and re-layouts  11.1 us (12%)
  other arithmetic  3.86 us (4%)
  matrix products  3.86 us (4%)
  between operations  1.02 us (1%)
    all_to_all x1, waiting for transfers between devices, on_device(): recv = lax.all_to_all(payload, 'tile', 0, 0, tiled=True)  38.8 us
    ppermute x1, starting transfers between devices, with_halo(): lax.ppermute(jnp.where(odd, tail, head), axis, [(i, (i + 1) % count if i...  19.6 us
    all_to_all x1, starting transfers between devices, on_device(): recv = lax.all_to_all(payload, 'tile', 0, 0, tiled=True)  14.4 us
    unnamed x15, local copies, waits for them, and re-layouts  4.67 us
    dot_general x1, matrix products, on_device(): jnp.einsum('sbk,brkt->brst', snapped, weights, preferred_element_type=jnp...  2.87 us
    ppermute x1, starting transfers between devices, with_halo(): lax.ppermute(jnp.where(odd, head, tail), axis, [(i, i ^ 1) for i in range...  1.92 us
  transfers between devices with their start and end apart: 3, of which 1 were waited for; matrix products, arithmetic and copies ran while one was open for 5% of the time, Pallas kernels for 0%

profile of v3, /device:TPU:32, one launch (start us, length us, event | category | flops | bytes accessed | tf_op | source)
XLA Modules:
  0.0 94.4 jit_solution(3457167987584656779)
XLA Ops:
  0.6 0.9 constant_dynamic-update-slice_fusion.1
  1.5 0.8 bitcast_dynamic-update-slice_fusion.2
  2.3 0.8 bitcast_dynamic-update-slice_fusion.1
  3.1 0.8 bitcast_dynamic-update-slice_fusion
  3.8 0.8 constant_dynamic-update-slice_fusion
  4.7 1.9 %collective-permute-start = (f32[8,4,256]{2,1,0:T(4,128)S(1)}, f32[8,4,256]{2,1,0:T(4,128)S(1)}, u32[]{:S(2)}, u32[]{:S(2)}) collective-permute-start(f32[8,4,256]{2,1,0:T(4,128)S(1)} %get-tuple-element.55), channel_id=1, source_target_pairs={{0,8},{8,0},{16,24},{24,16},{32,40},{40,32},{48,56},{56,48},{64,72... | collective-permute-start | bytes 98312 | tf_op jit(solution)/shard_map/ppermute | solution.py:21
  6.6 19.6 %collective-permute-start.1 = (f32[8,4,256]{2,1,0:T(4,128)S(1)}, f32[8,4,256]{2,1,0:T(4,128)S(1)}, u32[]{:S(2)}, u32[]{:S(2)}) collective-permute-start(f32[8,4,256]{2,1,0:T(4,128)S(1)} %get-tuple-element.56), channel_id=1, source_target_pairs={{0,504},{8,16},{16,8},{24,32},{32,24},{40,48},{48,40},{56,64},{64,... | collective-permute-start | bytes 98312 | tf_op jit(solution)/shard_map/ppermute | solution.py:24
  26.2 0.8 slice_bitcast_fusion.15
  27.0 0.7 convert_add_fusion
  27.9 0.8 copy.30
  28.8 0.2 convert_reduce_fusion
  29.1 0.3 fusion.3
  29.5 0.8 slice.831
  34.0 2.9 %fusion.5 = f32[64,4,2,128]{3,1,2,0:T(4,128)S(1)} fusion(bf16[64,2,128,128]{3,2,1,0:T(8,128)(2,1)} %param.15, bf16[1,64,128]{2,0,1:T(2,128)(2,1)S(1)} %stack.62, bf16[1,64,128]{2,0,1:T(2,128)(2,1)S(1)} %stack.61, bf16[1,64,128]{2,0,1:T(2,128)(2,1)S(1)} %stack.60, bf16[1,64,128]{2,0,1:T(2,128)(2,1)S(1)} %stack.59), kind=kOutput, calls=%fused_computation.12 | convolution fusion | flops 17039360 | bytes 4521984 | tf_op jit(solution)/shard_map/sbk,brkt->brst/dot_general | solution.py:100
  36.9 0.4 fusion
  37.3 0.2 reshape.144
  37.6 1.2 %all_to_all.8 = f32[64,1,2176]{2,1,0:T(1,128)} reshape(f32[64,2176]{1,0:T(8,128)S(1)} %select_maximum_fusion) | data formatting | bytes 1114112 | tf_op jit(solution)/shard_map/all_to_all | solution.py:123
  38.7 14.4 %all-to-all-start = ((f32[64,1,2176]{2,1,0:T(1,128)}), f32[64,1,2176]{2,1,0:T(1,128)S(1)}, u32[]{:S(2)}, u32[]{:S(2)}) async-start(f32[64,1,2176]{2,1,0:T(1,128)} %all_to_all.8), calls=%async_computation | async-start | bytes 1114112 | tf_op jit(solution)/shard_map/all_to_all | solution.py:123
  53.5 0.6 pad_maximum_fusion.1
  54.1 38.8 %all-to-all-done = f32[64,1,2176]{2,1,0:T(1,128)S(1)} async-done(((f32[64,1,2176]{2,1,0:T(1,128)}), f32[64,1,2176]{2,1,0:T(1,128)S(1)}, u32[]{:S(2)}, u32[]{:S(2)}) %all-to-all-start) | async-done | bytes 557088 | tf_op jit(solution)/shard_map/all_to_all | solution.py:123
  93.1 0.1 reshape.145
  93.2 0.2 copy.36
  93.4 0.3 fusion.108
  93.8 0.7 copy.37
  (79 shorter events, 4.6 us)
Async XLA Ops:
  4.7 25.7 %collective-permute-start = (f32[8,4,256]{2,1,0:T(4,128)S(1)}, f32[8,4,256]{2,1,0:T(4,128)S(1)}, u32[]{:S(2)}, u32[]{:S(2)}) collective-permute-start(f32[8,4,256]{2,1,0:T(4,128)S(1)} %get-tuple-element.55), channel_id=1, source_target_pairs={{0,8},{8,0},{16,24},{24,16},{32,40},{40,32},{48,56},{56,48},{64,72... | collective-permute-start | bytes 98312 | tf_op jit(solution)/shard_map/ppermute | solution.py:21
  6.6 23.7 %collective-permute-start.1 = (f32[8,4,256]{2,1,0:T(4,128)S(1)}, f32[8,4,256]{2,1,0:T(4,128)S(1)}, u32[]{:S(2)}, u32[]{:S(2)}) collective-permute-start(f32[8,4,256]{2,1,0:T(4,128)S(1)} %get-tuple-element.56), channel_id=1, source_target_pairs={{0,504},{8,16},{16,8},{24,32},{32,24},{40,48},{48,40},{56,64},{64,... | collective-permute-start | bytes 98312 | tf_op jit(solution)/shard_map/ppermute | solution.py:24
  31.1 2.5 %copy-start = (f32[32,256]{1,0:T(8,128)S(1)}, f32[32,256]{1,0:T(8,128)}, u32[]{:S(2)}) copy-start(f32[32,256]{1,0:T(8,128)} %param.9) | copy-start | bytes 98308
  31.3 2.5 %copy-start.1 = (f32[2,32,256]{2,1,0:T(8,128)S(1)}, f32[2,32,256]{2,1,0:T(8,128)}, u32[]{:S(2)}) copy-start(f32[2,32,256]{2,1,0:T(8,128)} %param.12) | copy-start | bytes 196612
  31.4 2.4 %copy-start.2 = (f32[32,256]{1,0:T(8,128)S(1)}, f32[32,256]{1,0:T(8,128)}, u32[]{:S(2)}) copy-start(f32[32,256]{1,0:T(8,128)} %param.11) | copy-start | bytes 98308
  34.0 19.4 %copy-start.3 = (f32[32,256]{1,0:T(8,128)S(1)}, f32[32,256]{1,0:T(8,128)}, u32[]{:S(2)}) copy-start(f32[32,256]{1,0:T(8,128)} %param.10) | copy-start | bytes 98308
  38.7 54.1 %all-to-all-start = ((f32[64,1,2176]{2,1,0:T(1,128)}), f32[64,1,2176]{2,1,0:T(1,128)S(1)}, u32[]{:S(2)}, u32[]{:S(2)}) async-start(f32[64,1,2176]{2,1,0:T(1,128)} %all_to_all.8), calls=%async_computation | async-start | bytes 1114112 | tf_op jit(solution)/shard_map/all_to_all | solution.py:123

commit v4 on v2

--- a/solution.py
+++ b/solution.py
@@ -11,20 +11,20 @@
 time_step = 0.3
 
 
-def with_halo(cells, sides, width):
-    for axis, dim in sides:
-        count = lax.axis_size(axis)
-        head = lax.slice_in_dim(cells, 0, width, axis=dim)
-        tail = lax.slice_in_dim(cells, cells.shape[dim] - width, cells.shape[dim], axis=dim)
-        cells = jnp.concatenate(
-            [
-                lax.ppermute(tail, axis, [(i, (i + 1) % count) for i in range(count)]),
-                cells,
-                lax.ppermute(head, axis, [((i + 1) % count, i) for i in range(count)]),
-            ],
-            axis=dim,
+def halo_pair(head, tail, axis):
+    count = lax.axis_size(axis)
+    if count % 2 == 0:
+        odd = lax.axis_index(axis) % 2 == 1
+        near = lax.ppermute(jnp.where(odd, head, tail), axis, [(i, i ^ 1) for i in range(count)])
+        far = lax.ppermute(
+            jnp.where(odd, tail, head),
+            axis,
+            [(i, (i + 1) % count if i % 2 else (i - 1) % count) for i in range(count)],
         )
-    return cells
+        return jnp.where(odd, near, far), jnp.where(odd, far, near)
+    before = lax.ppermute(tail, axis, [(i, (i + 1) % count) for i in range(count)])
+    after = lax.ppermute(head, axis, [((i + 1) % count, i) for i in range(count)])
+    return before, after
 
 
 def advance(fields, metric):
@@ -76,25 +76,10 @@
 
 
 def on_device(initial, depth_field, coriolis, cell_area, face_len, owners, offsets, weights):
-    cells = jnp.concatenate(
-        [initial, jnp.stack([depth_field, coriolis, cell_area]), face_len], axis=0
-    )
-    cells_ext = with_halo(cells, (("tile", 1),), STEPS)
-    width = cells_ext.shape[1]
-    fields = cells_ext[:3]
-    snapshots = []
-    for number in range(STEPS):
-        metric_ext = cells_ext[3:, number : width - number]
-        fields = advance(fields, metric_ext)
-        keep = STEPS - 1 - number
-        snapshots.append(fields[0, keep : fields.shape[1] - keep])
-    snapped = jnp.stack(snapshots).astype(jnp.bfloat16).reshape(STEPS, -1, 128)
-    contribution = jnp.einsum(
-        "sbk,brkt->brst", snapped, weights, preferred_element_type=jnp.float32
-    )
+    pieces = [initial, depth_field[None], coriolis[None], cell_area[None], face_len]
+    width = STEPS
+    n_tile = lax.axis_size("tile")
     slot_count = weights.shape[0] * weights.shape[1]
-    flat = contribution.reshape(slot_count, STEPS * 128)
-    n_tile = lax.axis_size("tile")
     item = jnp.arange(slot_count, dtype=jnp.int32)
     own_owner = owners.reshape(-1)
     same = own_owner[:, None] == own_owner[None, :]
@@ -103,7 +88,6 @@
     pack = (jnp.arange(n_tile * CAP, dtype=jnp.int32)[:, None] == slot[None, :]).astype(
         jnp.float32
     )
-    send = jnp.dot(pack, flat, precision=lax.Precision.HIGHEST, preferred_element_type=jnp.float32)
     labels = jnp.dot(
         pack,
         offsets.reshape(-1, 1).astype(jnp.float32) + 1.0,
@@ -111,6 +95,25 @@
         preferred_element_type=jnp.float32,
     ).reshape(n_tile, CAP) - 1.0
     label_row = jnp.pad(labels, ((0, 0), (0, 128 - CAP)))
+    head = jnp.concatenate([p[:, :width] for p in pieces], axis=0)
+    tail = jnp.concatenate([p[:, p.shape[1] - width :] for p in pieces], axis=0)
+    head, tail, pack, label_row = lax.optimization_barrier((head, tail, pack, label_row))
+    before, after = halo_pair(head, tail, "tile")
+    cells_ext = jnp.concatenate([before, jnp.concatenate(pieces, axis=0), after], axis=1)
+    full = cells_ext.shape[1]
+    fields = cells_ext[:3]
+    snapshots = []
+    for number in range(STEPS):
+        metric_ext = cells_ext[3:, number : full - number]
+        fields = advance(fields, metric_ext)
+        keep = STEPS - 1 - number
+        snapshots.append(fields[0, keep : fields.shape[1] - keep])
+    snapped = jnp.stack(snapshots).astype(jnp.bfloat16).reshape(STEPS, -1, 128)
+    contribution = jnp.einsum(
+        "sbk,brkt->brst", snapped, weights, preferred_element_type=jnp.float32
+    )
+    flat = contribution.reshape(slot_count, STEPS * 128)
+    send = jnp.dot(pack, flat, precision=lax.Precision.HIGHEST, preferred_element_type=jnp.float32)
     payload = jnp.concatenate([send.reshape(n_tile, CAP * STEPS * 128), label_row], axis=1)
     recv = lax.all_to_all(payload, "tile", 0, 0, tiled=True)
     recv_data = recv[:, : CAP * STEPS * 128].reshape(n_tile * CAP, STEPS * 128)

time: 94.2 us -> 98 us (1.040)
  local copies, waits for them, and re-layouts: 11.1 us -> 14.8 us
    unnamed x15 -> x19, local copies, waits for them, and re-layouts: 4.67 us -> 7.61 us
    all_to_all x1, starting transfers between devices: 14.4 us -> 12.9 us  [on_device(): recv = lax.all_to_all(payload, 'tile', 0, 0, tiled=True)]
  transfers between devices with their start and end apart: 3 -> 3, of which waited for: 1 -> 1; matrix products, arithmetic and copies ran while one was open for 5% -> 7% of each run, Pallas kernels for 0% -> 0%
where the time goes in v4:
time: 98 us; the launch traced here: 96.9 us
  waiting for transfers between devices  38.8 us (40%)
  starting transfers between devices  34.4 us (35%)
  local copies, waits for them, and re-layouts  14.8 us (15%)
  matrix products  4.03 us (4%)
  other arithmetic  3.88 us (4%)
  between operations  1.05 us (1%)
    all_to_all x1, waiting for transfers between devices, on_device(): recv = lax.all_to_all(payload, 'tile', 0, 0, tiled=True)  38.8 us
    ppermute x1, starting transfers between devices, halo_pair(): lax.ppermute(jnp.where(odd, tail, head), axis, [(i, (i + 1) % count if i...  19.6 us
    all_to_all x1, starting transfers between devices, on_device(): recv = lax.all_to_all(payload, 'tile', 0, 0, tiled=True)  12.9 us
    unnamed x19, local copies, waits for them, and re-layouts  7.61 us
    dot_general x1, matrix products, on_device(): jnp.einsum('sbk,brkt->brst', snapped, weights, preferred_element_type=jnp...  2.87 us
  transfers between devices with their start and end apart: 3, of which 1 were waited for; matrix products, arithmetic and copies ran while one was open for 7% of the time, Pallas kernels for 0%

profile of v4, /device:TPU:32, one launch (start us, length us, event | category | flops | bytes accessed | tf_op | source)
XLA Modules:
  0.0 96.9 jit_solution(14303777673740580578)
XLA Ops:
  0.7 0.7 convert_add_fusion
  1.6 0.8 copy.30
  3.2 0.8 constant_dynamic-update-slice_fusion.9
  4.0 0.7 constant_dynamic-update-slice_fusion.8
  4.7 0.7 constant_dynamic-update-slice_fusion.7
  5.5 0.7 constant_dynamic-update-slice_fusion.6
  6.2 0.7 constant_dynamic-update-slice_fusion.5
  6.9 1.9 %collective-permute-start = (f32[8,4,256]{2,1,0:T(4,128)S(1)}, f32[8,4,256]{2,1,0:T(4,128)S(1)}, u32[]{:S(2)}, u32[]{:S(2)}) collective-permute-start(f32[8,4,256]{2,1,0:T(4,128)S(1)} %bitcast.328), channel_id=1, source_target_pairs={{0,8},{8,0},{16,24},{24,16},{32,40},{40,32},{48,56},{56,48},{64,72... | collective-permute-start | bytes 98312 | tf_op jit(solution)/shard_map/ppermute | solution.py:18
  8.9 19.6 %collective-permute-start.1 = (f32[8,4,256]{2,1,0:T(4,128)S(1)}, f32[8,4,256]{2,1,0:T(4,128)S(1)}, u32[]{:S(2)}, u32[]{:S(2)}) collective-permute-start(f32[8,4,256]{2,1,0:T(4,128)S(1)} %bitcast.326), channel_id=1, source_target_pairs={{0,504},{8,16},{16,8},{24,32},{32,24},{40,48},{48,40},{56,64},{64,... | collective-permute-start | bytes 98312 | tf_op jit(solution)/shard_map/ppermute | solution.py:19
  28.5 0.8 slice_bitcast_fusion.15
  29.2 0.9 constant_dynamic-update-slice_fusion.14
  30.1 0.8 constant_dynamic-update-slice_fusion.13
  30.9 0.8 constant_dynamic-update-slice_fusion.12
  31.6 0.8 constant_dynamic-update-slice_fusion.11
  32.4 0.8 constant_dynamic-update-slice_fusion.10
  33.2 0.8 slice.863
  37.7 2.9 %fusion.6 = f32[64,4,2,128]{3,1,2,0:T(4,128)S(1)} fusion(bf16[64,2,128,128]{3,2,1,0:T(8,128)(2,1)} %param.15, bf16[1,64,128]{2,0,1:T(2,128)(2,1)S(1)} %stack.50, bf16[1,64,128]{2,0,1:T(2,128)(2,1)S(1)} %stack.49, bf16[1,64,128]{2,0,1:T(2,128)(2,1)S(1)} %stack.48, bf16[1,64,128]{2,0,1:T(2,128)(2,1)S(1)} %stack.47), kind=kOutput, calls=%fused_computation.12 | convolution fusion | flops 17039360 | bytes 4521984 | tf_op jit(solution)/shard_map/sbk,brkt->brst/dot_general | solution.py:112
  40.6 0.6 fusion
  41.5 1.2 %all_to_all.8 = f32[64,1,2176]{2,1,0:T(1,128)} reshape(f32[64,2176]{1,0:T(8,128)S(1)} %pad_maximum_fusion) | data formatting | bytes 1114112 | tf_op jit(solution)/shard_map/all_to_all | solution.py:118
  42.6 12.9 %all-to-all-start = ((f32[64,1,2176]{2,1,0:T(1,128)}), f32[64,1,2176]{2,1,0:T(1,128)S(1)}, u32[]{:S(2)}, u32[]{:S(2)}) async-start(f32[64,1,2176]{2,1,0:T(1,128)} %all_to_all.8), calls=%async_computation | async-start | bytes 1114112 | tf_op jit(solution)/shard_map/all_to_all | solution.py:118
  55.9 0.6 pad_maximum_fusion.2
  56.6 38.8 %all-to-all-done = f32[64,1,2176]{2,1,0:T(1,128)S(1)} async-done(((f32[64,1,2176]{2,1,0:T(1,128)}), f32[64,1,2176]{2,1,0:T(1,128)S(1)}, u32[]{:S(2)}, u32[]{:S(2)}) %all-to-all-start) | async-done | bytes 557088 | tf_op jit(solution)/shard_map/all_to_all | solution.py:118
  95.9 0.3 fusion.108
  96.2 0.7 copy.37
  (86 shorter events, 5.6 us)
Async XLA Ops:
  6.9 27.1 %collective-permute-start = (f32[8,4,256]{2,1,0:T(4,128)S(1)}, f32[8,4,256]{2,1,0:T(4,128)S(1)}, u32[]{:S(2)}, u32[]{:S(2)}) collective-permute-start(f32[8,4,256]{2,1,0:T(4,128)S(1)} %bitcast.328), channel_id=1, source_target_pairs={{0,8},{8,0},{16,24},{24,16},{32,40},{40,32},{48,56},{56,48},{64,72... | collective-permute-start | bytes 98312 | tf_op jit(solution)/shard_map/ppermute | solution.py:18
  8.9 25.2 %collective-permute-start.1 = (f32[8,4,256]{2,1,0:T(4,128)S(1)}, f32[8,4,256]{2,1,0:T(4,128)S(1)}, u32[]{:S(2)}, u32[]{:S(2)}) collective-permute-start(f32[8,4,256]{2,1,0:T(4,128)S(1)} %bitcast.326), channel_id=1, source_target_pairs={{0,504},{8,16},{16,8},{24,32},{32,24},{40,48},{48,40},{56,64},{64,... | collective-permute-start | bytes 98312 | tf_op jit(solution)/shard_map/ppermute | solution.py:19
  34.9 2.5 %copy-start = (f32[32,256]{1,0:T(8,128)S(1)}, f32[32,256]{1,0:T(8,128)}, u32[]{:S(2)}) copy-start(f32[32,256]{1,0:T(8,128)} %param.9) | copy-start | bytes 98308
  35.0 2.5 %copy-start.1 = (f32[2,32,256]{2,1,0:T(8,128)S(1)}, f32[2,32,256]{2,1,0:T(8,128)}, u32[]{:S(2)}) copy-start(f32[2,32,256]{2,1,0:T(8,128)} %param.12) | copy-start | bytes 196612
  35.2 2.4 %copy-start.2 = (f32[32,256]{1,0:T(8,128)S(1)}, f32[32,256]{1,0:T(8,128)}, u32[]{:S(2)}) copy-start(f32[32,256]{1,0:T(8,128)} %param.11) | copy-start | bytes 98308
  37.7 18.1 %copy-start.3 = (f32[32,256]{1,0:T(8,128)S(1)}, f32[32,256]{1,0:T(8,128)}, u32[]{:S(2)}) copy-start(f32[32,256]{1,0:T(8,128)} %param.10) | copy-start | bytes 98308
  42.6 52.7 %all-to-all-start = ((f32[64,1,2176]{2,1,0:T(1,128)}), f32[64,1,2176]{2,1,0:T(1,128)S(1)}, u32[]{:S(2)}, u32[]{:S(2)}) async-start(f32[64,1,2176]{2,1,0:T(1,128)} %all_to_all.8), calls=%async_computation | async-start | bytes 1114112 | tf_op jit(solution)/shard_map/all_to_all | solution.py:118

commit v5 on v3

--- a/solution.py
+++ b/solution.py
@@ -2,10 +2,14 @@
 import jax.numpy as jnp
 from jax import lax
 from jax.sharding import PartitionSpec as P
+from jax.experimental import pallas as pl
+from jax.experimental.pallas import tpu as pltpu
 
 STEPS = 4
 TB = 16
 CAP = 4
+HALO = 8
+CHANNELS = 8
 
 
 time_step = 0.3
@@ -83,20 +87,141 @@
     return jnp.stack([new_h, new_u, new_v])
 
 
+def edge_kernel(odd_ref, ini_h, ini_t, dep_h, dep_t, cor_h, cor_t, area_h, area_t, face_h, face_t, near_ref, far_ref):
+    odd = odd_ref[0] == 1
+    head = [ini_h[0], ini_h[1], ini_h[2], dep_h[...], cor_h[...], area_h[...], face_h[0], face_h[1]]
+    tail = [ini_t[0], ini_t[1], ini_t[2], dep_t[...], cor_t[...], area_t[...], face_t[0], face_t[1]]
+    for c in range(CHANNELS):
+        near_ref[c] = jnp.where(odd, head[c], tail[c])
+        far_ref[c] = jnp.where(odd, tail[c], head[c])
+
+
+def edges(odd, initial, depth_field, coriolis, cell_area, face_len):
+    rows, lanes = depth_field.shape
+    last = rows // HALO - 1
+    spec3 = lambda b: pl.BlockSpec((3, HALO, lanes), lambda i: (0, b, 0))
+    spec2 = lambda b: pl.BlockSpec((HALO, lanes), lambda i: (b, 0))
+    specf = lambda b: pl.BlockSpec((2, HALO, lanes), lambda i: (0, b, 0))
+    out = jax.ShapeDtypeStruct((CHANNELS, HALO, lanes), jnp.float32)
+    return pl.pallas_call(
+        edge_kernel,
+        out_shape=(out, out),
+        in_specs=[
+            pl.BlockSpec(memory_space=pltpu.SMEM),
+            spec3(0), spec3(last), spec2(0), spec2(last), spec2(0), spec2(last),
+            spec2(0), spec2(last), specf(0), specf(last),
+        ],
+        out_specs=(
+            pl.BlockSpec((CHANNELS, HALO, lanes), lambda i: (0, 0, 0)),
+            pl.BlockSpec((CHANNELS, HALO, lanes), lambda i: (0, 0, 0)),
+        ),
+        grid=(1,),
+    )(odd, initial, initial, depth_field, depth_field, coriolis, coriolis, cell_area, cell_area, face_len, face_len)
+
+
+def stencil_kernel(ini, dep, cor, area, face, before, after, final_ref, snap_ref, ext):
+    own_rows = ini.shape[1]
+    owns = [ini[0], ini[1], ini[2], dep[...], cor[...], area[...], face[0], face[1]]
+    for c in range(CHANNELS):
+        ext[c, :HALO] = before[c]
+        ext[c, HALO : HALO + own_rows] = owns[c]
+        ext[c, HALO + own_rows :] = after[c]
+    rows, lanes = ext.shape[1], ext.shape[2]
+    lane = lax.broadcasted_iota(jnp.int32, (rows, lanes), 1)
+    top = lane == lanes - 1
+    bottom = lane == 0
+
+    def east(x):
+        return pltpu.roll(x, rows - 1, 0)
+
+    def west(x):
+        return pltpu.roll(x, 1, 0)
+
+    def up(x):
+        return pltpu.roll(x, lanes - 1, 1)
+
+    def down(x):
+        return pltpu.roll(x, 1, 1)
+
+    depth, rotation, cell, east_len, north_len = (ext[c] for c in range(3, CHANNELS))
+    wave_x = jnp.sqrt(jnp.maximum(depth, east(depth)))
+    depth_e = east(depth)
+    depth_up = jnp.where(top, depth, up(depth))
+    wave_y = jnp.sqrt(jnp.maximum(depth, depth_up))
+    root_d = jnp.sqrt(depth)
+    factor = time_step / cell
+    height, speed_x, speed_y = ext[0], ext[1], ext[2]
+    for number in range(STEPS):
+        h_e, u_e, v_e = east(height), east(speed_x), east(speed_y)
+        flux_h = east_len * (
+            0.5 * (depth * speed_x + depth_e * u_e) - 0.5 * wave_x * (h_e - height)
+        )
+        flux_u = east_len * (0.5 * (height + h_e) - 0.5 * wave_x * (u_e - speed_x))
+        flux_v = east_len * (-0.5 * wave_x * (v_e - speed_y))
+        h_up = jnp.where(top, height, up(height))
+        u_up = jnp.where(top, speed_x, up(speed_x))
+        v_up = jnp.where(top, -speed_y, up(speed_y))
+        north_h = north_len * (
+            0.5 * (depth * speed_y + depth_up * v_up) - 0.5 * wave_y * (h_up - height)
+        )
+        north_u = north_len * (-0.5 * wave_y * (u_up - speed_x))
+        north_v = north_len * (0.5 * (height + h_up) - 0.5 * wave_y * (v_up - speed_y))
+        wall_v = north_len * (height - root_d * speed_y)
+        south_h = jnp.where(bottom, 0.0, down(north_h))
+        south_u = jnp.where(bottom, 0.0, down(north_u))
+        south_v = jnp.where(bottom, wall_v, down(north_v))
+        new_h = height - factor * (flux_h - west(flux_h) + north_h - south_h)
+        new_u = (
+            speed_x
+            - factor * (flux_u - west(flux_u) + north_u - south_u)
+            + time_step * rotation * speed_y
+        )
+        new_v = (
+            speed_y
+            - factor * (flux_v - west(flux_v) + north_v - south_v)
+            - time_step * rotation * speed_x
+        )
+        height, speed_x, speed_y = new_h, new_u, new_v
+        snap_ref[number] = height[HALO : HALO + own_rows].astype(snap_ref.dtype)
+    final_ref[0] = height[HALO : HALO + own_rows]
+    final_ref[1] = speed_x[HALO : HALO + own_rows]
+    final_ref[2] = speed_y[HALO : HALO + own_rows]
+
+
+def stencil(initial, depth_field, coriolis, cell_area, face_len, before, after):
+    rows, lanes = depth_field.shape
+    whole = lambda shape: pl.BlockSpec(shape, lambda: (0,) * len(shape))
+    return pl.pallas_call(
+        stencil_kernel,
+        out_shape=(
+            jax.ShapeDtypeStruct((3, rows, lanes), jnp.float32),
+            jax.ShapeDtypeStruct((STEPS, rows, lanes), jnp.bfloat16),
+        ),
+        in_specs=[
+            whole(initial.shape), whole(depth_field.shape), whole(coriolis.shape),
+            whole(cell_area.shape), whole(face_len.shape), whole(before.shape), whole(after.shape),
+        ],
+        out_specs=(whole((3, rows, lanes)), whole((STEPS, rows, lanes))),
+        scratch_shapes=[pltpu.VMEM((CHANNELS, rows + 2 * HALO, lanes), jnp.float32)],
+    )(initial, depth_field, coriolis, cell_area, face_len, before, after)
+
+
+def halo_exchange(near, far, axis):
+    count = lax.axis_size(axis)
+    odd = lax.axis_index(axis) % 2 == 1
+    near_in = lax.ppermute(near, axis, [(i, i ^ 1) for i in range(count)])
+    far_in = lax.ppermute(
+        far, axis, [(i, (i + 1) % count if i % 2 else (i - 1) % count) for i in range(count)]
+    )
+    return jnp.where(odd, near_in, far_in), jnp.where(odd, far_in, near_in)
+
+
 def on_device(initial, depth_field, coriolis, cell_area, face_len, owners, offsets, weights):
-    cells = jnp.concatenate(
-        [initial, jnp.stack([depth_field, coriolis, cell_area]), face_len], axis=0
-    )
-    cells_ext = with_halo(cells, (("tile", 1),), STEPS)
-    width = cells_ext.shape[1]
-    fields = cells_ext[:3]
-    snapshots = []
-    for number in range(STEPS):
-        metric_ext = cells_ext[3:, number : width - number]
-        fields = advance(fields, metric_ext)
-        keep = STEPS - 1 - number
-        snapshots.append(fields[0, keep : fields.shape[1] - keep])
-    snapped = jnp.stack(snapshots).astype(jnp.bfloat16).reshape(STEPS, -1, 128)
+    odd = (lax.axis_index("tile") % 2).astype(jnp.int32).reshape(1)
+    near, far = edges(odd, initial, depth_field, coriolis, cell_area, face_len)
+    before, after = halo_exchange(near, far, "tile")
+    fields, snaps = stencil(initial, depth_field, coriolis, cell_area, face_len, before, after)
+    snapped = snaps.reshape(STEPS, -1, 128)
     contribution = jnp.einsum(
         "sbk,brkt->brst", snapped, weights, preferred_element_type=jnp.float32
     )

time: 95.3 us -> 93.6 us (0.982)
  blocking collectives: 0 us -> 55.6 us
  waiting for transfers between devices: 38.8 us -> 1.64 us
  starting transfers between devices: 35.8 us -> 21.5 us
  local copies, waits for them, and re-layouts: 11.1 us -> 3.91 us
  Pallas kernels: 0 us -> 4.02 us
  other arithmetic: 3.86 us -> 1.72 us
    all_to_all x0 -> x1, blocking collectives: none -> 55.6 us  [on_device(): recv = lax.all_to_all(payload, 'tile', 0, 0, tiled=True)]
    all_to_all x1 -> x0, waiting for transfers between devices: 38.8 us -> none  [on_device(): recv = lax.all_to_all(payload, 'tile', 0, 0, tiled=True)]
    all_to_all x1 -> x0, starting transfers between devices: 14.4 us -> none  [on_device(): recv = lax.all_to_all(payload, 'tile', 0, 0, tiled=True)]
    pallas_call x0 -> x2, Pallas kernels: none -> 4.02 us  [the longest x1 2.49 us: stencil(): pl.pallas_call(stencil_kernel, out_shape=(jax.ShapeDtypeStruct((3, rows,...]
    unnamed x15 -> x3, local copies, waits for them, and re-layouts: 4.67 us -> 1.47 us
    slice x27 -> x0, local copies, waits for them, and re-layouts: 3.12 us -> none  [the longest x4 1.06 us: advance(): above_d = jnp.concatenate([own_d[:, 1:], own_d[:, -1:]], axis=1)]
    ppermute x2, waiting for transfers between devices: 0.01 us -> 1.64 us  [the longest x1 1.64 us: halo_exchange(): lax.ppermute(far, axis, [(i, (i + 1) % count if i % 2 else (i - 1) % coun...]
    mul x16 -> x0, other arithmetic: 1.32 us -> none  [the longest x4 0.4 us: advance(): north_u = own_n * (-0.5 * wave_y * (above_u - own_u))]
  transfers between devices with their start and end apart: 3 -> 2, of which waited for: 1 -> 1; matrix products, arithmetic and copies ran while one was open for 5% -> 3% of each run, Pallas kernels for 0% -> 0%
where the time goes in v5:
time: 93.6 us; the launch traced here: 93 us
  blocking collectives  55.6 us (59%)
  starting transfers between devices  21.5 us (23%)
  Pallas kernels  4.02 us (4%)
  local copies, waits for them, and re-layouts  3.91 us (4%)
  matrix products  3.82 us (4%)
  other arithmetic  1.72 us (2%)
  waiting for transfers between devices  1.64 us (2%)
    all_to_all x1, blocking collectives, on_device(): recv = lax.all_to_all(payload, 'tile', 0, 0, tiled=True)  55.6 us
    ppermute x1, starting transfers between devices, halo_exchange(): lax.ppermute(far, axis, [(i, (i + 1) % count if i % 2 else (i - 1) % coun...  19.6 us
    dot_general x1, matrix products, on_device(): jnp.einsum('sbk,brkt->brst', snapped, weights, preferred_element_type=jnp...  2.84 us
    pallas_call x1, Pallas kernels, stencil(): pl.pallas_call(stencil_kernel, out_shape=(jax.ShapeDtypeStruct((3, rows,...  2.49 us
    ppermute x1, starting transfers between devices, halo_exchange(): near_in = lax.ppermute(near, axis, [(i, i ^ 1) for i in range(count)])  1.91 us
  transfers between devices with their start and end apart: 2, of which 1 were waited for; matrix products, arithmetic and copies ran while one was open for 3% of the time, Pallas kernels for 0%

profile of v5, /device:TPU:32, one launch (start us, length us, event | category | flops | bytes accessed | tf_op | source)
XLA Modules:
  0.0 93.0 jit_solution(12630567027181191971)
XLA Ops:
  0.6 1.5 %shard_map.95 = (f32[8,8,256]{2,1,0:T(8,128)}, f32[8,8,256]{2,1,0:T(8,128)}) custom-call(s32[1]{0:T(128)} %bitcast.odd_ref, f32[3,32,256]{2,1,0:T(8,128)} %ini.1, f32[3,32,256]{2,1,0:T(8,128)} %ini.1, f32[32,256]{1,0:T(8,128)} %dep.1, f32[32,256]{1,0:T(8,128)} %dep.1, f32[32,256]{1,0:T(8,128)} %cor.1, f32[32,256]{1,0:T(8,128)} %cor.1, f32[32,256]{1,0:T(8,128)} %area.1, ...), custom_call_target="tpu_custom_call" | custom-call | tf_op jit(solution)/shard_map/pallas_call | solution.py:106
  2.2 1.9 %collective-permute-start = (f32[8,8,256]{2,1,0:T(8,128)}, f32[8,8,256]{2,1,0:T(8,128)S(1)}, u32[]{:S(2)}, u32[]{:S(2)}) collective-permute-start(f32[8,8,256]{2,1,0:T(8,128)} %get-tuple-element.6), channel_id=1, source_target_pairs={{0,8},{8,0},{16,24},{24,16},{32,40},{40,32},{48,56},{56,48},{64,72... | collective-permute-start | bytes 196616 | tf_op jit(solution)/shard_map/ppermute | solution.py:212
  4.1 19.6 %collective-permute-start.1 = (f32[8,8,256]{2,1,0:T(8,128)}, f32[8,8,256]{2,1,0:T(8,128)S(1)}, u32[]{:S(2)}, u32[]{:S(2)}) collective-permute-start(f32[8,8,256]{2,1,0:T(8,128)} %get-tuple-element.7), channel_id=1, source_target_pairs={{0,504},{8,16},{16,8},{24,32},{32,24},{40,48},{48,40},{56,64},{64,... | collective-permute-start | bytes 196616 | tf_op jit(solution)/shard_map/ppermute | solution.py:213
  23.7 0.7 convert_add_fusion
  24.5 0.1 reshape.73
  24.6 0.8 copy.25
  25.4 0.1 reshape.66
  25.5 0.2 convert_reduce_fusion
  25.7 0.1 broadcast_compare_fusion
  25.8 0.3 fusion.3
  26.2 1.6 %collective-permute-done.1 = f32[8,8,256]{2,1,0:T(8,128)S(1)} collective-permute-done((f32[8,8,256]{2,1,0:T(8,128)}, f32[8,8,256]{2,1,0:T(8,128)S(1)}, u32[]{:S(2)}, u32[]{:S(2)}) %collective-permute-start.1) | collective-permute-done | bytes 65568 | tf_op jit(solution)/shard_map/ppermute | solution.py:213
  27.9 0.7 broadcast_select_fusion
  28.5 2.5 %shard_map.96 = (f32[3,32,256]{2,1,0:T(8,128)}, bf16[4,32,256]{2,1,0:T(8,128)(2,1)}) custom-call(f32[3,32,256]{2,1,0:T(8,128)} %ini.1, f32[32,256]{1,0:T(8,128)} %dep.1, f32[32,256]{1,0:T(8,128)} %cor.1, f32[32,256]{1,0:T(8,128)} %area.1, f32[2,32,256]{2,1,0:T(8,128)} %face.1, f32[8,8,256]{2,1,0:T(8,128)} %get-tuple-element.19.before, ...), custom_call_target="tpu_custom_call" | custom-call | tf_op jit(solution)/shard_map/pallas_call | solution.py:194
  31.0 0.9 reshape.68
  31.9 2.8 %fusion.5 = f32[64,4,2,128]{3,1,2,0:T(4,128)S(1)} fusion(bf16[64,2,128,128]{3,2,1,0:T(8,128)(2,1)} %param.15, bf16[4,64,128,1]{2,1,0,3:T(8,128)(2,1)S(1)} %bitcast.26), kind=kOutput, calls=%fused_computation.9 | convolution fusion | flops 16777216 | bytes 4521984 | tf_op jit(solution)/shard_map/sbk,brkt->brst/dot_general | solution.py:225
  34.7 0.4 fusion
  35.1 0.2 reshape.70
  35.4 0.4 all_to_all.8
  35.8 55.6 %all_to_all.12 = f32[64,1,2176]{2,1,0:T(1,128)S(1)} all-to-all(f32[64,1,2176]{2,1,0:T(1,128)S(1)} %all_to_all.8), channel_id=1, replica_groups=mesh['tile'=64,'exp'=8] {'tile'}, dimensions={0} | all-to-all | bytes 1114112 | tf_op jit(solution)/shard_map/all_to_all | solution.py:248
  91.5 0.1 eq.77
  91.6 0.1 reshape.71
  91.8 0.2 copy.28
  92.0 0.3 fusion.10
  92.3 0.7 copy.29
  (10 shorter events, 0.3 us)
Async XLA Ops:
  2.2 24.1 %collective-permute-start = (f32[8,8,256]{2,1,0:T(8,128)}, f32[8,8,256]{2,1,0:T(8,128)S(1)}, u32[]{:S(2)}, u32[]{:S(2)}) collective-permute-start(f32[8,8,256]{2,1,0:T(8,128)} %get-tuple-element.6), channel_id=1, source_target_pairs={{0,8},{8,0},{16,24},{24,16},{32,40},{40,32},{48,56},{56,48},{64,72... | collective-permute-start | bytes 196616 | tf_op jit(solution)/shard_map/ppermute | solution.py:212
  4.1 23.8 %collective-permute-start.1 = (f32[8,8,256]{2,1,0:T(8,128)}, f32[8,8,256]{2,1,0:T(8,128)S(1)}, u32[]{:S(2)}, u32[]{:S(2)}) collective-permute-start(f32[8,8,256]{2,1,0:T(8,128)} %get-tuple-element.7), channel_id=1, source_target_pairs={{0,504},{8,16},{16,8},{24,32},{32,24},{40,48},{48,40},{56,64},{64,... | collective-permute-start | bytes 196616 | tf_op jit(solution)/shard_map/ppermute | solution.py:213

commit v6 on v5

--- a/solution.py
+++ b/solution.py
@@ -119,13 +119,14 @@
     )(odd, initial, initial, depth_field, depth_field, coriolis, coriolis, cell_area, cell_area, face_len, face_len)
 
 
-def stencil_kernel(ini, dep, cor, area, face, before, after, final_ref, snap_ref, ext):
+def stencil_kernel(odd_ref, ini, dep, cor, area, face, near_in, far_in, final_ref, snap_ref, ext):
     own_rows = ini.shape[1]
+    odd = odd_ref[0] == 1
     owns = [ini[0], ini[1], ini[2], dep[...], cor[...], area[...], face[0], face[1]]
     for c in range(CHANNELS):
-        ext[c, :HALO] = before[c]
+        ext[c, :HALO] = jnp.where(odd, near_in[c], far_in[c])
         ext[c, HALO : HALO + own_rows] = owns[c]
-        ext[c, HALO + own_rows :] = after[c]
+        ext[c, HALO + own_rows :] = jnp.where(odd, far_in[c], near_in[c])
     rows, lanes = ext.shape[1], ext.shape[2]
     lane = lax.broadcasted_iota(jnp.int32, (rows, lanes), 1)
     top = lane == lanes - 1
@@ -182,28 +183,33 @@
             - time_step * rotation * speed_x
         )
         height, speed_x, speed_y = new_h, new_u, new_v
-        snap_ref[number] = height[HALO : HALO + own_rows].astype(snap_ref.dtype)
+        for half in range(lanes // 128):
+            snap_ref[number, half] = height[
+                HALO : HALO + own_rows, half * 128 : (half + 1) * 128
+            ].astype(snap_ref.dtype)
     final_ref[0] = height[HALO : HALO + own_rows]
     final_ref[1] = speed_x[HALO : HALO + own_rows]
     final_ref[2] = speed_y[HALO : HALO + own_rows]
 
 
-def stencil(initial, depth_field, coriolis, cell_area, face_len, before, after):
+def stencil(odd, initial, depth_field, coriolis, cell_area, face_len, near_in, far_in):
     rows, lanes = depth_field.shape
     whole = lambda shape: pl.BlockSpec(shape, lambda: (0,) * len(shape))
+    snap_shape = (STEPS, lanes // 128, rows, 128)
     return pl.pallas_call(
         stencil_kernel,
         out_shape=(
             jax.ShapeDtypeStruct((3, rows, lanes), jnp.float32),
-            jax.ShapeDtypeStruct((STEPS, rows, lanes), jnp.bfloat16),
+            jax.ShapeDtypeStruct(snap_shape, jnp.bfloat16),
         ),
         in_specs=[
+            pl.BlockSpec(memory_space=pltpu.SMEM),
             whole(initial.shape), whole(depth_field.shape), whole(coriolis.shape),
-            whole(cell_area.shape), whole(face_len.shape), whole(before.shape), whole(after.shape),
+            whole(cell_area.shape), whole(face_len.shape), whole(near_in.shape), whole(far_in.shape),
         ],
-        out_specs=(whole((3, rows, lanes)), whole((STEPS, rows, lanes))),
+        out_specs=(whole((3, rows, lanes)), whole(snap_shape)),
         scratch_shapes=[pltpu.VMEM((CHANNELS, rows + 2 * HALO, lanes), jnp.float32)],
-    )(initial, depth_field, coriolis, cell_area, face_len, before, after)
+    )(odd, initial, depth_field, coriolis, cell_area, face_len, near_in, far_in)
 
 
 def halo_exchange(near, far, axis):
@@ -213,17 +219,18 @@
     far_in = lax.ppermute(
         far, axis, [(i, (i + 1) % count if i % 2 else (i - 1) % count) for i in range(count)]
     )
-    return jnp.where(odd, near_in, far_in), jnp.where(odd, far_in, near_in)
+    return near_in, far_in
 
 
 def on_device(initial, depth_field, coriolis, cell_area, face_len, owners, offsets, weights):
     odd = (lax.axis_index("tile") % 2).astype(jnp.int32).reshape(1)
     near, far = edges(odd, initial, depth_field, coriolis, cell_area, face_len)
-    before, after = halo_exchange(near, far, "tile")
-    fields, snaps = stencil(initial, depth_field, coriolis, cell_area, face_len, before, after)
-    snapped = snaps.reshape(STEPS, -1, 128)
+    near_in, far_in = halo_exchange(near, far, "tile")
+    fields, snaps = stencil(odd, initial, depth_field, coriolis, cell_area, face_len, near_in, far_in)
+    halves = snaps.shape[1]
+    grouped = weights.reshape((-1, halves) + weights.shape[1:])
     contribution = jnp.einsum(
-        "sbk,brkt->brst", snapped, weights, preferred_element_type=jnp.float32
+        "shck,chrkt->chrst", snaps, grouped, preferred_element_type=jnp.float32
     )
     slot_count = weights.shape[0] * weights.shape[1]
     flat = contribution.reshape(slot_count, STEPS * 128)
@@ -251,10 +258,14 @@
     unpack = (
         recv_offset[None, :] == jnp.arange(TB, dtype=jnp.float32)[:, None]
     ).astype(jnp.float32)
-    gathered = jnp.dot(
-        unpack, recv_data, precision=lax.Precision.HIGHEST, preferred_element_type=jnp.float32
-    )
-    return (gathered.reshape(TB, STEPS, 128), fields)
+    gathered = jnp.einsum(
+        "tq,qsk->tsk",
+        unpack,
+        recv_data.reshape(n_tile * CAP, STEPS, 128),
+        precision=lax.Precision.HIGHEST,
+        preferred_element_type=jnp.float32,
+    )
+    return (gathered, fields)
 
 
 def solution(mesh):

time: 93.6 us -> 92.6 us (0.989)
    reshape x3 -> x0, local copies, waits for them, and re-layouts: 1.21 us -> none  [the longest x1 0.87 us: on_device(): snapped = snaps.reshape(STEPS, -1, 128)]
    unnamed x3 -> x7, local copies, waits for them, and re-layouts: 1.47 us -> 2.06 us
where the time goes in v6:
time: 92.6 us; the launch traced here: 92.1 us
  blocking collectives  55.6 us (60%)
  starting transfers between devices  21.5 us (23%)
  Pallas kernels  4.02 us (4%)
  matrix products  3.83 us (4%)
  local copies, waits for them, and re-layouts  3.65 us (4%)
  waiting for transfers between devices  1.64 us (2%)
  other arithmetic  1.06 us (1%)
    all_to_all x1, blocking collectives, on_device(): recv = lax.all_to_all(payload, 'tile', 0, 0, tiled=True)  55.6 us
    ppermute x1, starting transfers between devices, halo_exchange(): lax.ppermute(far, axis, [(i, (i + 1) % count if i % 2 else (i - 1) % coun...  19.6 us
    dot_general x1, matrix products, on_device(): jnp.einsum('shck,chrkt->chrst', snaps, grouped, preferred_element_type=jn...  2.88 us
    pallas_call x1, Pallas kernels, stencil(): pl.pallas_call(stencil_kernel, out_shape=(jax.ShapeDtypeStruct((3, rows,...  2.49 us
    unnamed x7, local copies, waits for them, and re-layouts  2.06 us
    ppermute x1, starting transfers between devices, halo_exchange(): near_in = lax.ppermute(near, axis, [(i, i ^ 1) for i in range(count)])  1.91 us
  transfers between devices with their start and end apart: 2, of which 1 were waited for; matrix products, arithmetic and copies ran while one was open for 3% of the time, Pallas kernels for 0%

profile of v6, /device:TPU:32, one launch (start us, length us, event | category | flops | bytes accessed | tf_op | source)
XLA Modules:
  0.0 92.1 jit_solution(2610455857343685504)
XLA Ops:
  0.6 1.5 %shard_map.95 = (f32[8,8,256]{2,1,0:T(8,128)}, f32[8,8,256]{2,1,0:T(8,128)}) custom-call(s32[1]{0:T(128)} %bitcast.odd_ref, f32[3,32,256]{2,1,0:T(8,128)} %ini.1, f32[3,32,256]{2,1,0:T(8,128)} %ini.1, f32[32,256]{1,0:T(8,128)} %dep.1, f32[32,256]{1,0:T(8,128)} %dep.1, f32[32,256]{1,0:T(8,128)} %cor.1, f32[32,256]{1,0:T(8,128)} %cor.1, f32[32,256]{1,0:T(8,128)} %area.1, ...), custom_call_target="tpu_custom_call" | custom-call | tf_op jit(solution)/shard_map/pallas_call | solution.py:106
  2.2 1.9 %collective-permute-start = (f32[8,8,256]{2,1,0:T(8,128)}, f32[8,8,256]{2,1,0:T(8,128)S(1)}, u32[]{:S(2)}, u32[]{:S(2)}) collective-permute-start(f32[8,8,256]{2,1,0:T(8,128)} %get-tuple-element.6), channel_id=1, source_target_pairs={{0,8},{8,0},{16,24},{24,16},{32,40},{40,32},{48,56},{56,48},{64,72... | collective-permute-start | bytes 196616 | tf_op jit(solution)/shard_map/ppermute | solution.py:218
  4.1 19.6 %collective-permute-start.1 = (f32[8,8,256]{2,1,0:T(8,128)}, f32[8,8,256]{2,1,0:T(8,128)S(1)}, u32[]{:S(2)}, u32[]{:S(2)}) collective-permute-start(f32[8,8,256]{2,1,0:T(8,128)} %get-tuple-element.7), channel_id=1, source_target_pairs={{0,504},{8,16},{16,8},{24,32},{32,24},{40,48},{48,40},{56,64},{64,... | collective-permute-start | bytes 196616 | tf_op jit(solution)/shard_map/ppermute | solution.py:219
  23.7 0.7 convert_add_fusion
  24.4 0.1 copy.26
  24.5 0.1 reshape.67
  24.6 0.8 copy.24
  25.4 0.1 reshape.61
  25.5 0.2 convert_reduce_fusion
  25.7 0.1 broadcast_compare_fusion
  25.9 0.3 fusion.5
  26.1 0.1 copy.31
  26.3 1.6 %collective-permute-done.1.far_in = f32[8,8,256]{2,1,0:T(8,128)S(1)} collective-permute-done((f32[8,8,256]{2,1,0:T(8,128)}, f32[8,8,256]{2,1,0:T(8,128)S(1)}, u32[]{:S(2)}, u32[]{:S(2)}) %collective-permute-start.1) | collective-permute-done | bytes 65568 | tf_op jit(solution)/shard_map/ppermute | solution.py:219
  27.9 0.6 copy-done.1
  28.5 2.5 %shard_map.96 = (f32[3,32,256]{2,1,0:T(8,128)}, bf16[4,2,32,128]{3,2,1,0:T(8,128)(2,1)}) custom-call(s32[1]{0:T(128)} %bitcast.odd_ref, f32[3,32,256]{2,1,0:T(8,128)} %ini.1, f32[32,256]{1,0:T(8,128)} %dep.1, f32[32,256]{1,0:T(8,128)} %cor.1, f32[32,256]{1,0:T(8,128)} %area.1, f32[2,32,256]{2,1,0:T(8,128)} %face.1, f32[8,8,256]{2,1,0:T(8,128)} %copy-done, ...), custom_call_target="tpu_custom_call" | custom-call | tf_op jit(solution)/shard_map/pallas_call | solution.py:199
  31.0 2.9 %fusion.7 = f32[32,2,4,2,128]{4,2,3,1,0:T(4,128)S(1)} fusion(bf16[32,2,2,128,128]{4,3,2,1,0:T(8,128)(2,1)} %bitcast.19, bf16[4,2,32,128,1]{3,2,1,0,4:T(8,128)(2,1)} %bitcast.23), kind=kOutput, calls=%fused_computation.11 | convolution fusion | flops 16777216 | bytes 4521984 | tf_op jit(solution)/shard_map/shck,chrkt->chrst/dot_general | solution.py:232
  33.9 0.4 fusion.2
  34.3 0.2 reshape.65
  34.6 0.4 all_to_all.8
  35.0 55.6 %all_to_all.12 = f32[64,1,2176]{2,1,0:T(1,128)S(1)} all-to-all(f32[64,1,2176]{2,1,0:T(1,128)S(1)} %all_to_all.8), channel_id=1, replica_groups=mesh['tile'=64,'exp'=8] {'tile'}, dimensions={0} | all-to-all | bytes 1114112 | tf_op jit(solution)/shard_map/all_to_all | solution.py:255
  90.7 0.1 eq.72
  90.8 0.4 reshape_reshape.3
  91.1 0.3 fusion
  91.4 0.6 copy.28
  (11 shorter events, 0.2 us)
Async XLA Ops:
  2.2 24.1 %collective-permute-start = (f32[8,8,256]{2,1,0:T(8,128)}, f32[8,8,256]{2,1,0:T(8,128)S(1)}, u32[]{:S(2)}, u32[]{:S(2)}) collective-permute-start(f32[8,8,256]{2,1,0:T(8,128)} %get-tuple-element.6), channel_id=1, source_target_pairs={{0,8},{8,0},{16,24},{24,16},{32,40},{40,32},{48,56},{56,48},{64,72... | collective-permute-start | bytes 196616 | tf_op jit(solution)/shard_map/ppermute | solution.py:218
  4.1 23.8 %collective-permute-start.1 = (f32[8,8,256]{2,1,0:T(8,128)}, f32[8,8,256]{2,1,0:T(8,128)S(1)}, u32[]{:S(2)}, u32[]{:S(2)}) collective-permute-start(f32[8,8,256]{2,1,0:T(8,128)} %get-tuple-element.7), channel_id=1, source_target_pairs={{0,504},{8,16},{16,8},{24,32},{32,24},{40,48},{48,40},{56,64},{64,... | collective-permute-start | bytes 196616 | tf_op jit(solution)/shard_map/ppermute | solution.py:219
  26.2 1.6 %copy-start = (f32[8,8,256]{2,1,0:T(8,128)}, f32[8,8,256]{2,1,0:T(8,128)S(1)}, u32[]{:S(2)}) copy-start(f32[8,8,256]{2,1,0:T(8,128)S(1)} %collective-permute-done.near_in) | copy-start | bytes 196612
  27.9 0.6 copy-start.1

commit v7 on v6

--- a/solution.py
+++ b/solution.py
@@ -226,11 +226,24 @@
     odd = (lax.axis_index("tile") % 2).astype(jnp.int32).reshape(1)
     near, far = edges(odd, initial, depth_field, coriolis, cell_area, face_len)
     near_in, far_in = halo_exchange(near, far, "tile")
+    halves = initial.shape[2] // 128
+    grouped = weights.reshape((-1, halves) + weights.shape[1:])
+    columns = initial.shape[1]
+    lo, hi = STEPS, columns - STEPS
+
+    def contribute(snaps, first, last):
+        return jnp.einsum(
+            "shck,chrkt->chrst",
+            snaps[:, :, first:last],
+            grouped[first:last],
+            preferred_element_type=jnp.float32,
+        )
+
+    _, inner_snaps = stencil(odd, initial, depth_field, coriolis, cell_area, face_len, near, far)
+    inner = contribute(inner_snaps, lo, hi)
     fields, snaps = stencil(odd, initial, depth_field, coriolis, cell_area, face_len, near_in, far_in)
-    halves = snaps.shape[1]
-    grouped = weights.reshape((-1, halves) + weights.shape[1:])
-    contribution = jnp.einsum(
-        "shck,chrkt->chrst", snaps, grouped, preferred_element_type=jnp.float32
+    contribution = jnp.concatenate(
+        [contribute(snaps, 0, lo), inner, contribute(snaps, hi, columns)], axis=0
     )
     slot_count = weights.shape[0] * weights.shape[1]
     flat = contribution.reshape(slot_count, STEPS * 128)

time: 92.6 us -> 93.8 us (1.013)
  blocking collectives: 55.6 us -> 51.6 us
  local copies, waits for them, and re-layouts: 3.65 us -> 7.61 us
  Pallas kernels: 4.02 us -> 6.53 us
  waiting for transfers between devices: 1.64 us -> 0.01 us
    all_to_all x1, blocking collectives: 55.6 us -> 51.6 us  [on_device(): recv = lax.all_to_all(payload, 'tile', 0, 0, tiled=True)]
    pallas_call x1 -> x2, Pallas kernels: 2.49 us -> 4.99 us  [stencil(): pl.pallas_call(stencil_kernel, out_shape=(jax.ShapeDtypeStruct((3, rows,...]
    unnamed x7 -> x17, local copies, waits for them, and re-layouts: 2.06 us -> 4.17 us
    slice x0 -> x5, local copies, waits for them, and re-layouts: none -> 1.85 us  [the longest x3 1.09 us: contribute(): grouped[first:last]]
    ppermute x1, waiting for transfers between devices: 1.63 us -> 0.01 us  [halo_exchange(): lax.ppermute(far, axis, [(i, (i + 1) % count if i % 2 else (i - 1) % coun...]
    dot_general x1 -> x3, matrix products: 2.88 us -> 2.96 us  [contribute(): jnp.einsum('shck,chrkt->chrst', snaps[:, :, first:last], grouped[first:la...]
  transfers between devices with their start and end apart: 2 -> 2, of which waited for: 1 -> 0; matrix products, arithmetic and copies ran while one was open for 3% -> 3% of each run, Pallas kernels for 0% -> 3%
where the time goes in v7:
time: 93.8 us; the launch traced here: 93.1 us
  blocking collectives  51.6 us (55%)
  starting transfers between devices  21.5 us (23%)
  local copies, waits for them, and re-layouts  7.61 us (8%)
  Pallas kernels  6.53 us (7%)
  matrix products  4.53 us (5%)
    all_to_all x1, blocking collectives, on_device(): recv = lax.all_to_all(payload, 'tile', 0, 0, tiled=True)  51.6 us
    ppermute x1, starting transfers between devices, halo_exchange(): lax.ppermute(far, axis, [(i, (i + 1) % count if i % 2 else (i - 1) % coun...  19.6 us
    pallas_call x2, Pallas kernels, stencil(): pl.pallas_call(stencil_kernel, out_shape=(jax.ShapeDtypeStruct((3, rows,...  4.99 us
    unnamed x17, local copies, waits for them, and re-layouts  4.17 us
    dot_general x3, matrix products, contribute(): jnp.einsum('shck,chrkt->chrst', snaps[:, :, first:last], grouped[first:la...  2.96 us
    ppermute x1, starting transfers between devices, halo_exchange(): near_in = lax.ppermute(near, axis, [(i, i ^ 1) for i in range(count)])  1.91 us
  transfers between devices with their start and end apart: 2, of which 0 were waited for; matrix products, arithmetic and copies ran while one was open for 3% of the time, Pallas kernels for 3%

profile of v7, /device:TPU:32, one launch (start us, length us, event | category | flops | bytes accessed | tf_op | source)
XLA Modules:
  0.0 93.1 jit_solution(8756546550524082891)
XLA Ops:
  0.6 1.5 %shard_map.95 = (f32[8,8,256]{2,1,0:T(8,128)}, f32[8,8,256]{2,1,0:T(8,128)}) custom-call(s32[1]{0:T(128)} %bitcast.odd_ref, f32[3,32,256]{2,1,0:T(8,128)} %ini.3, f32[3,32,256]{2,1,0:T(8,128)} %ini.3, f32[32,256]{1,0:T(8,128)} %dep.3, f32[32,256]{1,0:T(8,128)} %dep.3, f32[32,256]{1,0:T(8,128)} %cor.3, f32[32,256]{1,0:T(8,128)} %cor.3, f32[32,256]{1,0:T(8,128)} %area.3, ...), custom_call_target="tpu_custom_call" | custom-call | tf_op jit(solution)/shard_map/pallas_call | solution.py:106
  2.2 1.9 %collective-permute-start = (f32[8,8,256]{2,1,0:T(8,128)}, f32[8,8,256]{2,1,0:T(8,128)S(1)}, u32[]{:S(2)}, u32[]{:S(2)}) collective-permute-start(f32[8,8,256]{2,1,0:T(8,128)} %get-tuple-element.7.near_in), channel_id=1, source_target_pairs={{0,8},{8,0},{16,24},{24,16},{32,40},{40,32},{48,56},{56,48},{64,72... | collective-permute-start | bytes 196616 | tf_op jit(solution)/shard_map/ppermute | solution.py:218
  4.1 19.6 %collective-permute-start.1 = (f32[8,8,256]{2,1,0:T(8,128)}, f32[8,8,256]{2,1,0:T(8,128)S(1)}, u32[]{:S(2)}, u32[]{:S(2)}) collective-permute-start(f32[8,8,256]{2,1,0:T(8,128)} %get-tuple-element.8.far_in), channel_id=1, source_target_pairs={{0,504},{8,16},{16,8},{24,32},{32,24},{40,48},{48,40},{56,64},{64,... | collective-permute-start | bytes 196616 | tf_op jit(solution)/shard_map/ppermute | solution.py:219
  23.7 2.5 %shard_map.97 = (f32[3,32,256]{2,1,0:T(8,128)}, bf16[4,2,32,128]{3,2,1,0:T(8,128)(2,1)}) custom-call(s32[1]{0:T(128)} %bitcast.odd_ref, f32[3,32,256]{2,1,0:T(8,128)} %ini.3, f32[32,256]{1,0:T(8,128)} %dep.3, f32[32,256]{1,0:T(8,128)} %cor.3, f32[32,256]{1,0:T(8,128)} %area.3, f32[2,32,256]{2,1,0:T(8,128)} %face.3, f32[8,8,256]{2,1,0:T(8,128)} %get-tuple-element.7.near_in, ...), custom_call_target="tpu_custom_call" | custom-call | tf_op jit(solution)/shard_map/pallas_call | solution.py:199
  26.2 2.2 %copy-done = bf16[64,2,128,128]{3,2,1,0:T(8,128)(2,1)S(1)} copy-done((bf16[64,2,128,128]{3,2,1,0:T(8,128)(2,1)S(1)}, bf16[64,2,128,128]{3,2,1,0:T(8,128)(2,1)}, u32[]{:S(2)}) %copy-start) | copy-done | bytes 4194328
  28.4 1.1 %fusion.15 = (bf16[8,2,128,128]{3,2,1,0:T(8,128)(2,1)}, bf16[8,2,128,128]{3,2,1,0:T(8,128)(2,1)}) fusion(bf16[64,2,128,128]{3,2,1,0:T(8,128)(2,1)S(1)} %copy-done), kind=kLoop, calls=%fused_computation.33 | loop fusion | bytes 2097152 | tf_op jit(solution)/shard_map/slice | solution.py:238
  29.6 0.1 reshape.62
  29.7 0.2 convert_reduce_fusion
  30.1 0.1 reshape.69
  30.3 0.3 fusion.5
  30.7 0.5 convolution_bitcast_fusion
  31.3 0.6 copy-done.1
  31.9 0.6 copy-done.2
  32.5 2.5 %shard_map.96 = (f32[3,32,256]{2,1,0:T(8,128)}, bf16[4,2,32,128]{3,2,1,0:T(8,128)(2,1)}) custom-call(s32[1]{0:T(128)} %bitcast.odd_ref, f32[3,32,256]{2,1,0:T(8,128)} %ini.3, f32[32,256]{1,0:T(8,128)} %dep.3, f32[32,256]{1,0:T(8,128)} %cor.3, f32[32,256]{1,0:T(8,128)} %area.3, f32[2,32,256]{2,1,0:T(8,128)} %face.3, f32[8,8,256]{2,1,0:T(8,128)} %copy-done.1, ...), custom_call_target="tpu_custom_call" | custom-call | tf_op jit(solution)/shard_map/pallas_call | solution.py:199
  35.0 0.7 slice_bitcast_fusion.2
  35.7 1.2 %convolution_bitcast_fusion.2 = f32[4,2,2,4,128]{4,3,2,1,0:T(4,128)S(1)} fusion(bf16[4,2,2,128,128]{4,3,2,1,0:T(8,128)(2,1)} %bitcast.37, bf16[4,2,4,128,1]{3,2,1,0,4:T(4,128)(2,1)S(1)} %get-tuple-element.22), kind=kOutput, calls=%fused_computation.2 | convolution fusion | flops 2097152 | bytes 565248 | tf_op jit(solution)/shard_map/shck,chrkt->chrst/dot_general | solution.py:235
  37.0 1.2 %convolution_bitcast_fusion.1 = f32[4,2,2,4,128]{4,3,2,1,0:T(4,128)S(1)} fusion(bf16[4,2,2,128,128]{4,3,2,1,0:T(8,128)(2,1)} %bitcast.36, bf16[4,2,4,128,1]{3,2,1,0,4:T(4,128)(2,1)S(1)} %get-tuple-element.23), kind=kOutput, calls=%fused_computation.1 | convolution fusion | flops 2097152 | bytes 565248 | tf_op jit(solution)/shard_map/shck,chrkt->chrst/dot_general | solution.py:235
  38.3 1.0 %fusion.2 = f32[256,512]{1,0:T(8,128)S(1)} fusion(f32[16,8,4,128]{3,2,1,0:T(4,128)S(1)} %bitcast.38, s32[128]{0:T(128)} %copy-done.4), kind=kOutput, calls=%fused_computation.8 | convolution fusion | flops 201359360 | bytes 786944 | tf_op jit(solution)/shard_map/dot_general | solution.py:259
  39.3 0.2 reshape.65
  39.6 0.4 all_to_all.8
  40.0 51.6 %all_to_all.12 = f32[64,1,2176]{2,1,0:T(1,128)S(1)} all-to-all(f32[64,1,2176]{2,1,0:T(1,128)S(1)} %all_to_all.8), channel_id=1, replica_groups=mesh['tile'=64,'exp'=8] {'tile'}, dimensions={0} | all-to-all | bytes 1114112 | tf_op jit(solution)/shard_map/all_to_all | solution.py:268
  91.7 0.4 reshape_reshape.3
  92.2 0.3 fusion
  92.5 0.6 copy.36
  (30 shorter events, 0.8 us)
Async XLA Ops:
  2.2 29.1 %collective-permute-start = (f32[8,8,256]{2,1,0:T(8,128)}, f32[8,8,256]{2,1,0:T(8,128)S(1)}, u32[]{:S(2)}, u32[]{:S(2)}) collective-permute-start(f32[8,8,256]{2,1,0:T(8,128)} %get-tuple-element.7.near_in), channel_id=1, source_target_pairs={{0,8},{8,0},{16,24},{24,16},{32,40},{40,32},{48,56},{56,48},{64,72... | collective-permute-start | bytes 196616 | tf_op jit(solution)/shard_map/ppermute | solution.py:218
  4.1 27.2 %collective-permute-start.1 = (f32[8,8,256]{2,1,0:T(8,128)}, f32[8,8,256]{2,1,0:T(8,128)S(1)}, u32[]{:S(2)}, u32[]{:S(2)}) collective-permute-start(f32[8,8,256]{2,1,0:T(8,128)} %get-tuple-element.8.far_in), channel_id=1, source_target_pairs={{0,504},{8,16},{16,8},{24,32},{32,24},{40,48},{48,40},{56,64},{64,... | collective-permute-start | bytes 196616 | tf_op jit(solution)/shard_map/ppermute | solution.py:219
  26.2 2.2 %copy-start = (bf16[64,2,128,128]{3,2,1,0:T(8,128)(2,1)S(1)}, bf16[64,2,128,128]{3,2,1,0:T(8,128)(2,1)}, u32[]{:S(2)}) copy-start(bf16[64,2,128,128]{3,2,1,0:T(8,128)(2,1)} %param.15) | copy-start | bytes 12582916
  26.2 3.3 %copy-start.3 = (bf16[4,2,32,128]{3,2,1,0:T(8,128)(2,1)S(1)}, bf16[4,2,32,128]{3,2,1,0:T(8,128)(2,1)}, u32[]{:S(2)}) copy-start(bf16[4,2,32,128]{3,2,1,0:T(8,128)(2,1)} %get-tuple-element.10) | copy-start | bytes 196612
  26.2 3.3 %copy-start.5 = (s32[64,2]{0,1:T(2,128)S(1)}, s32[64,2]{0,1:T(2,128)}, u32[]{:S(2)}) copy-start(s32[64,2]{0,1:T(2,128)} %param.13) | copy-start | bytes 1540
  26.2 3.7 %copy-start.6 = (s32[64,2]{0,1:T(2,128)S(1)}, s32[64,2]{0,1:T(2,128)}, u32[]{:S(2)}) copy-start(s32[64,2]{0,1:T(2,128)} %param.14) | copy-start | bytes 1540
  26.2 4.5 %slice-start = ((bf16[64,2,128,128]{3,2,1,0:T(8,128)(2,1)}), bf16[48,2,128,128]{3,2,1,0:T(8,128)(2,1)S(1)}, s32[]{:S(2)}) async-start(bf16[64,2,128,128]{3,2,1,0:T(8,128)(2,1)} %param.15), calls=%async_computation.1 | async-start | bytes 6291456 | tf_op jit(solution)/shard_map/slice | solution.py:238
  29.9 0.8 copy-start.4
  31.3 0.6 copy-start.1
  31.9 0.6 copy-start.2

commit v8 on v6

--- a/solution.py
+++ b/solution.py
@@ -226,14 +226,22 @@
     odd = (lax.axis_index("tile") % 2).astype(jnp.int32).reshape(1)
     near, far = edges(odd, initial, depth_field, coriolis, cell_area, face_len)
     near_in, far_in = halo_exchange(near, far, "tile")
-    fields, snaps = stencil(odd, initial, depth_field, coriolis, cell_area, face_len, near_in, far_in)
-    halves = snaps.shape[1]
+    halves = initial.shape[2] // 128
     grouped = weights.reshape((-1, halves) + weights.shape[1:])
-    contribution = jnp.einsum(
-        "shck,chrkt->chrst", snaps, grouped, preferred_element_type=jnp.float32
-    )
+    columns = initial.shape[1]
+    lo, hi = STEPS, columns - STEPS
+    per_column = halves * weights.shape[1]
     slot_count = weights.shape[0] * weights.shape[1]
-    flat = contribution.reshape(slot_count, STEPS * 128)
+
+    def contribute(snaps, grouped_part):
+        part = jnp.einsum(
+            "shck,chrkt->chrst", snaps, grouped_part, preferred_element_type=jnp.float32
+        )
+        return part.reshape(-1, STEPS * 128)
+
+    _, inner_snaps = stencil(odd, initial, depth_field, coriolis, cell_area, face_len, near, far)
+    inner = contribute(inner_snaps[:, :, lo:hi], grouped[lo:hi])
+    edge_weights = jnp.concatenate([grouped[:lo], grouped[hi:]], axis=0)
     n_tile = lax.axis_size("tile")
     item = jnp.arange(slot_count, dtype=jnp.int32)
     own_owner = owners.reshape(-1)
@@ -243,7 +251,22 @@
     pack = (jnp.arange(n_tile * CAP, dtype=jnp.int32)[:, None] == slot[None, :]).astype(
         jnp.float32
     )
-    send = jnp.dot(pack, flat, precision=lax.Precision.HIGHEST, preferred_element_type=jnp.float32)
+    inner_send = jnp.dot(
+        pack[:, lo * per_column : hi * per_column],
+        inner,
+        precision=lax.Precision.HIGHEST,
+        preferred_element_type=jnp.float32,
+    )
+    fields, snaps = stencil(odd, initial, depth_field, coriolis, cell_area, face_len, near_in, far_in)
+    edge = contribute(
+        jnp.concatenate([snaps[:, :, :lo], snaps[:, :, hi:]], axis=2), edge_weights
+    )
+    edge_pack = jnp.concatenate(
+        [pack[:, : lo * per_column], pack[:, hi * per_column :]], axis=1
+    )
+    send = inner_send + jnp.dot(
+        edge_pack, edge, precision=lax.Precision.HIGHEST, preferred_element_type=jnp.float32
+    )
     labels = jnp.dot(
         pack,
         offsets.reshape(-1, 1).astype(jnp.float32) + 1.0,

time: 92.6 us -> 92.3 us (level)
  blocking collectives: 55.6 us -> 48 us
  local copies, waits for them, and re-layouts: 3.65 us -> 8.8 us
  Pallas kernels: 4.02 us -> 6.53 us
  waiting for transfers between devices: 1.64 us -> 0.01 us
    all_to_all x1, blocking collectives: 55.6 us -> 48 us  [on_device(): recv = lax.all_to_all(payload, 'tile', 0, 0, tiled=True)]
    pallas_call x1 -> x2, Pallas kernels: 2.49 us -> 4.99 us  [stencil(): pl.pallas_call(stencil_kernel, out_shape=(jax.ShapeDtypeStruct((3, rows,...]
    unnamed x7 -> x13, local copies, waits for them, and re-layouts: 2.06 us -> 4.17 us
    slice x0 -> x6, local copies, waits for them, and re-layouts: none -> 1.86 us  [the longest x1 1.08 us: on_device(): edge_weights = jnp.concatenate([grouped[:lo], grouped[hi:]], axis=0)]
    ppermute x1, waiting for transfers between devices: 1.63 us -> 0.01 us  [halo_exchange(): lax.ppermute(far, axis, [(i, (i + 1) % count if i % 2 else (i - 1) % coun...]
    add x2, local copies, waits for them, and re-layouts: 0.24 us -> 1.42 us  [on_device(): offsets.reshape(-1, 1).astype(jnp.float32) + 1.0]
    dot_general x2 -> x4, matrix products: 3.27 us -> 3.02 us  [the longest x2 1.97 us: contribute(): jnp.einsum('shck,chrkt->chrst', snaps, grouped_part, preferred_element_ty...]
  transfers between devices with their start and end apart: 2 -> 2, of which waited for: 1 -> 0; matrix products, arithmetic and copies ran while one was open for 3% -> 7% of each run, Pallas kernels for 0% -> 3%
where the time goes in v8:
time: 92.3 us; the launch traced here: 91.7 us
  blocking collectives  48 us (52%)
  starting transfers between devices  21.5 us (23%)
  local copies, waits for them, and re-layouts  8.8 us (10%)
  Pallas kernels  6.53 us (7%)
  matrix products  4.22 us (5%)
  other arithmetic  1.73 us (2%)
    all_to_all x1, blocking collectives, on_device(): recv = lax.all_to_all(payload, 'tile', 0, 0, tiled=True)  48 us
    ppermute x1, starting transfers between devices, halo_exchange(): lax.ppermute(far, axis, [(i, (i + 1) % count if i % 2 else (i - 1) % coun...  19.6 us
    pallas_call x2, Pallas kernels, stencil(): pl.pallas_call(stencil_kernel, out_shape=(jax.ShapeDtypeStruct((3, rows,...  4.99 us
    unnamed x13, local copies, waits for them, and re-layouts  4.17 us
    dot_general x2, matrix products, contribute(): jnp.einsum('shck,chrkt->chrst', snaps, grouped_part, preferred_element_ty...  1.97 us
    ppermute x1, starting transfers between devices, halo_exchange(): near_in = lax.ppermute(near, axis, [(i, i ^ 1) for i in range(count)])  1.91 us
  transfers between devices with their start and end apart: 2, of which 0 were waited for; matrix products, arithmetic and copies ran while one was open for 7% of the time, Pallas kernels for 3%

profile of v8, /device:TPU:32, one launch (start us, length us, event | category | flops | bytes accessed | tf_op | source)
XLA Modules:
  0.0 91.7 jit_solution(8374945058860085567)
XLA Ops:
  0.6 1.5 %shard_map.95 = (f32[8,8,256]{2,1,0:T(8,128)}, f32[8,8,256]{2,1,0:T(8,128)}) custom-call(s32[1]{0:T(128)} %bitcast.odd_ref, f32[3,32,256]{2,1,0:T(8,128)} %ini.3, f32[3,32,256]{2,1,0:T(8,128)} %ini.3, f32[32,256]{1,0:T(8,128)} %dep.3, f32[32,256]{1,0:T(8,128)} %dep.3, f32[32,256]{1,0:T(8,128)} %cor.3, f32[32,256]{1,0:T(8,128)} %cor.3, f32[32,256]{1,0:T(8,128)} %area.3, ...), custom_call_target="tpu_custom_call" | custom-call | tf_op jit(solution)/shard_map/pallas_call | solution.py:106
  2.2 1.9 %collective-permute-start = (f32[8,8,256]{2,1,0:T(8,128)}, f32[8,8,256]{2,1,0:T(8,128)S(1)}, u32[]{:S(2)}, u32[]{:S(2)}) collective-permute-start(f32[8,8,256]{2,1,0:T(8,128)} %get-tuple-element.7.near_in), channel_id=1, source_target_pairs={{0,8},{8,0},{16,24},{24,16},{32,40},{40,32},{48,56},{56,48},{64,72... | collective-permute-start | bytes 196616 | tf_op jit(solution)/shard_map/ppermute | solution.py:218
  4.1 19.6 %collective-permute-start.1 = (f32[8,8,256]{2,1,0:T(8,128)}, f32[8,8,256]{2,1,0:T(8,128)S(1)}, u32[]{:S(2)}, u32[]{:S(2)}) collective-permute-start(f32[8,8,256]{2,1,0:T(8,128)} %get-tuple-element.8.far_in), channel_id=1, source_target_pairs={{0,504},{8,16},{16,8},{24,32},{32,24},{40,48},{48,40},{56,64},{64,... | collective-permute-start | bytes 196616 | tf_op jit(solution)/shard_map/ppermute | solution.py:219
  23.7 2.5 %shard_map.96 = (f32[3,32,256]{2,1,0:T(8,128)}, bf16[4,2,32,128]{3,2,1,0:T(8,128)(2,1)}) custom-call(s32[1]{0:T(128)} %bitcast.odd_ref, f32[3,32,256]{2,1,0:T(8,128)} %ini.3, f32[32,256]{1,0:T(8,128)} %dep.3, f32[32,256]{1,0:T(8,128)} %cor.3, f32[32,256]{1,0:T(8,128)} %area.3, f32[2,32,256]{2,1,0:T(8,128)} %face.3, f32[8,8,256]{2,1,0:T(8,128)} %get-tuple-element.7.near_in, ...), custom_call_target="tpu_custom_call" | custom-call | tf_op jit(solution)/shard_map/pallas_call | solution.py:199
  26.2 2.2 %copy-done = bf16[64,2,128,128]{3,2,1,0:T(8,128)(2,1)S(1)} copy-done((bf16[64,2,128,128]{3,2,1,0:T(8,128)(2,1)S(1)}, bf16[64,2,128,128]{3,2,1,0:T(8,128)(2,1)}, u32[]{:S(2)}) %copy-start) | copy-done | bytes 4194328
  28.4 1.1 %fusion.27 = (bf16[8,2,128,128]{3,2,1,0:T(8,128)(2,1)}, bf16[8,2,128,128]{3,2,1,0:T(8,128)(2,1)}) fusion(bf16[64,2,128,128]{3,2,1,0:T(8,128)(2,1)S(1)} %copy-done), kind=kLoop, calls=%fused_computation.41 | loop fusion | bytes 2097152 | tf_op jit(solution)/shard_map/slice | solution.py:244
  30.2 1.2 %convert_add_fusion = f32[64,2]{0,1:T(2,128)} fusion(s32[64,2]{0,1:T(2,128)} %param.14), kind=kLoop, calls=%fused_computation.37 | loop fusion | flops 256 | bytes 1024 | tf_op jit(solution)/shard_map/add | solution.py:272
  31.4 0.8 copy.30
  32.2 0.7 reshape.72
  32.8 0.9 fusion.9
  33.9 0.5 fusion.15
  34.4 0.4 fusion.6
  34.9 0.6 copy-done.1
  35.5 0.6 copy-done.2
  36.1 2.5 %shard_map.97 = (f32[3,32,256]{2,1,0:T(8,128)}, bf16[4,2,32,128]{3,2,1,0:T(8,128)(2,1)}) custom-call(s32[1]{0:T(128)} %bitcast.odd_ref, f32[3,32,256]{2,1,0:T(8,128)} %ini.3, f32[32,256]{1,0:T(8,128)} %dep.3, f32[32,256]{1,0:T(8,128)} %cor.3, f32[32,256]{1,0:T(8,128)} %area.3, f32[2,32,256]{2,1,0:T(8,128)} %face.3, f32[8,8,256]{2,1,0:T(8,128)} %copy-done.1, ...), custom_call_target="tpu_custom_call" | custom-call | tf_op jit(solution)/shard_map/pallas_call | solution.py:199
  38.6 0.7 fusion.29
  39.4 1.5 %fusion = f32[8,2,2,128,4]{3,4,2,1,0:T(4,128)S(1)} fusion(bf16[4,2,2,128,128]{4,3,2,1,0:T(8,128)(2,1)} %bitcast.35, bf16[4,2,2,128,128]{4,3,2,1,0:T(8,128)(2,1)} %bitcast.34, bf16[4,2,8,128,1]{3,2,1,0,4:T(8,128)(2,1)S(1)} %maximum_bitcast_fusion), kind=kOutput, calls=%fused_computation.1 | convolution fusion | flops 4718592 | bytes 1130496 | tf_op jit(solution)/shard_map/shck,chrkt->chrst/dot_general | solution.py:237
  40.8 0.6 convolution_add_fusion
  41.4 0.2 reshape.69
  41.7 0.4 all_to_all.8
  42.1 48.0 %all_to_all.12 = f32[64,1,2176]{2,1,0:T(1,128)S(1)} all-to-all(f32[64,1,2176]{2,1,0:T(1,128)S(1)} %all_to_all.8), channel_id=1, replica_groups=mesh['tile'=64,'exp'=8] {'tile'}, dimensions={0} | all-to-all | bytes 1114112 | tf_op jit(solution)/shard_map/all_to_all | solution.py:278
  90.3 0.4 reshape_reshape.3
  90.7 0.3 fusion.4
  91.0 0.6 copy.32
  (28 shorter events, 1.0 us)
Async XLA Ops:
  2.2 32.7 %collective-permute-start = (f32[8,8,256]{2,1,0:T(8,128)}, f32[8,8,256]{2,1,0:T(8,128)S(1)}, u32[]{:S(2)}, u32[]{:S(2)}) collective-permute-start(f32[8,8,256]{2,1,0:T(8,128)} %get-tuple-element.7.near_in), channel_id=1, source_target_pairs={{0,8},{8,0},{16,24},{24,16},{32,40},{40,32},{48,56},{56,48},{64,72... | collective-permute-start | bytes 196616 | tf_op jit(solution)/shard_map/ppermute | solution.py:218
  4.1 30.8 %collective-permute-start.1 = (f32[8,8,256]{2,1,0:T(8,128)}, f32[8,8,256]{2,1,0:T(8,128)S(1)}, u32[]{:S(2)}, u32[]{:S(2)}) collective-permute-start(f32[8,8,256]{2,1,0:T(8,128)} %get-tuple-element.8.far_in), channel_id=1, source_target_pairs={{0,504},{8,16},{16,8},{24,32},{32,24},{40,48},{48,40},{56,64},{64,... | collective-permute-start | bytes 196616 | tf_op jit(solution)/shard_map/ppermute | solution.py:219
  26.2 2.2 %copy-start = (bf16[64,2,128,128]{3,2,1,0:T(8,128)(2,1)S(1)}, bf16[64,2,128,128]{3,2,1,0:T(8,128)(2,1)}, u32[]{:S(2)}) copy-start(bf16[64,2,128,128]{3,2,1,0:T(8,128)(2,1)} %param.15) | copy-start | bytes 12582916
  26.2 3.3 %copy-start.3 = (bf16[4,2,32,128]{3,2,1,0:T(8,128)(2,1)S(1)}, bf16[4,2,32,128]{3,2,1,0:T(8,128)(2,1)}, u32[]{:S(2)}) copy-start(bf16[4,2,32,128]{3,2,1,0:T(8,128)(2,1)} %get-tuple-element.9) | copy-start | bytes 196612
  26.2 3.3 %copy-start.4 = (s32[64,2]{0,1:T(2,128)S(1)}, s32[64,2]{0,1:T(2,128)}, u32[]{:S(2)}) copy-start(s32[64,2]{0,1:T(2,128)} %param.13) | copy-start | bytes 1540
  26.2 7.7 %slice-start = ((bf16[64,2,128,128]{3,2,1,0:T(8,128)(2,1)}), bf16[48,2,128,128]{3,2,1,0:T(8,128)(2,1)S(1)}, s32[]{:S(2)}) async-start(bf16[64,2,128,128]{3,2,1,0:T(8,128)(2,1)} %param.15), calls=%async_computation.1 | async-start | bytes 6291456 | tf_op jit(solution)/shard_map/slice | solution.py:243
  34.8 0.6 copy-start.1
  35.5 0.6 copy-start.2

commit v9 on v8

--- a/solution.py
+++ b/solution.py
@@ -119,7 +119,9 @@
     )(odd, initial, initial, depth_field, depth_field, coriolis, coriolis, cell_area, cell_area, face_len, face_len)
 
 
-def stencil_kernel(odd_ref, ini, dep, cor, area, face, near_in, far_in, final_ref, snap_ref, ext):
+def stencil_kernel(
+    odd_ref, ini, dep, cor, area, face, near_in, far_in, final_ref, snap_ref, edge_ref, ext
+):
     own_rows = ini.shape[1]
     odd = odd_ref[0] == 1
     owns = [ini[0], ini[1], ini[2], dep[...], cor[...], area[...], face[0], face[1]]
@@ -187,6 +189,11 @@
             snap_ref[number, half] = height[
                 HALO : HALO + own_rows, half * 128 : (half + 1) * 128
             ].astype(snap_ref.dtype)
+            rounded = height[:, half * 128 : (half + 1) * 128].astype(snap_ref.dtype)
+            edge_ref[number, half, :STEPS] = rounded[HALO : HALO + STEPS].astype(jnp.float32)
+            edge_ref[number, half, STEPS:] = rounded[
+                HALO + own_rows - STEPS : HALO + own_rows
+            ].astype(jnp.float32)
     final_ref[0] = height[HALO : HALO + own_rows]
     final_ref[1] = speed_x[HALO : HALO + own_rows]
     final_ref[2] = speed_y[HALO : HALO + own_rows]
@@ -196,18 +203,20 @@
     rows, lanes = depth_field.shape
     whole = lambda shape: pl.BlockSpec(shape, lambda: (0,) * len(shape))
     snap_shape = (STEPS, lanes // 128, rows, 128)
+    edge_shape = (STEPS, lanes // 128, 2 * STEPS, 128)
     return pl.pallas_call(
         stencil_kernel,
         out_shape=(
             jax.ShapeDtypeStruct((3, rows, lanes), jnp.float32),
             jax.ShapeDtypeStruct(snap_shape, jnp.bfloat16),
+            jax.ShapeDtypeStruct(edge_shape, jnp.float32),
         ),
         in_specs=[
             pl.BlockSpec(memory_space=pltpu.SMEM),
             whole(initial.shape), whole(depth_field.shape), whole(coriolis.shape),
             whole(cell_area.shape), whole(face_len.shape), whole(near_in.shape), whole(far_in.shape),
         ],
-        out_specs=(whole((3, rows, lanes)), whole(snap_shape)),
+        out_specs=(whole((3, rows, lanes)), whole(snap_shape), whole(edge_shape)),
         scratch_shapes=[pltpu.VMEM((CHANNELS, rows + 2 * HALO, lanes), jnp.float32)],
     )(odd, initial, depth_field, coriolis, cell_area, face_len, near_in, far_in)
 
@@ -239,7 +248,7 @@
         )
         return part.reshape(-1, STEPS * 128)
 
-    _, inner_snaps = stencil(odd, initial, depth_field, coriolis, cell_area, face_len, near, far)
+    _, inner_snaps, _ = stencil(odd, initial, depth_field, coriolis, cell_area, face_len, near, far)
     inner = contribute(inner_snaps[:, :, lo:hi], grouped[lo:hi])
     edge_weights = jnp.concatenate([grouped[:lo], grouped[hi:]], axis=0)
     n_tile = lax.axis_size("tile")
@@ -257,10 +266,10 @@
         precision=lax.Precision.HIGHEST,
         preferred_element_type=jnp.float32,
     )
-    fields, snaps = stencil(odd, initial, depth_field, coriolis, cell_area, face_len, near_in, far_in)
-    edge = contribute(
-        jnp.concatenate([snaps[:, :, :lo], snaps[:, :, hi:]], axis=2), edge_weights
-    )
+    fields, _, edge_snaps = stencil(
+        odd, initial, depth_field, coriolis, cell_area, face_len, near_in, far_in
+    )
+    edge = contribute(edge_snaps.astype(jnp.bfloat16), edge_weights)
     edge_pack = jnp.concatenate(
         [pack[:, : lo * per_column], pack[:, hi * per_column :]], axis=1
     )

time: 92.3 us -> 92.4 us (level)
  no operation moved by 1% of the time
where the time goes in v9:
time: 92.4 us; the launch traced here: 91.7 us
  blocking collectives  48 us (52%)
  starting transfers between devices  21.5 us (23%)
  local copies, waits for them, and re-layouts  8.06 us (9%)
  Pallas kernels  6.65 us (7%)
  matrix products  4.22 us (5%)
  other arithmetic  2.48 us (3%)
    all_to_all x1, blocking collectives, on_device(): recv = lax.all_to_all(payload, 'tile', 0, 0, tiled=True)  48 us
    ppermute x1, starting transfers between devices, halo_exchange(): lax.ppermute(far, axis, [(i, (i + 1) % count if i % 2 else (i - 1) % coun...  19.6 us
    pallas_call x2, Pallas kernels, stencil(): pl.pallas_call(stencil_kernel, out_shape=(jax.ShapeDtypeStruct((3, rows,...  5.1 us
    unnamed x13, local copies, waits for them, and re-layouts  4.17 us
    dot_general x2, matrix products, contribute(): jnp.einsum('shck,chrkt->chrst', snaps, grouped_part, preferred_element_ty...  1.97 us
    ppermute x1, starting transfers between devices, halo_exchange(): near_in = lax.ppermute(near, axis, [(i, i ^ 1) for i in range(count)])  1.91 us
  transfers between devices with their start and end apart: 2, of which 0 were waited for; matrix products, arithmetic and copies ran while one was open for 7% of the time, Pallas kernels for 3%

profile of v9, /device:TPU:32, one launch (start us, length us, event | category | flops | bytes accessed | tf_op | source)
XLA Modules:
  0.0 91.7 jit_solution(14840844499305816545)
XLA Ops:
  0.6 1.5 %shard_map.95 = (f32[8,8,256]{2,1,0:T(8,128)}, f32[8,8,256]{2,1,0:T(8,128)}) custom-call(s32[1]{0:T(128)} %bitcast.odd_ref, f32[3,32,256]{2,1,0:T(8,128)} %ini.3, f32[3,32,256]{2,1,0:T(8,128)} %ini.3, f32[32,256]{1,0:T(8,128)} %dep.3, f32[32,256]{1,0:T(8,128)} %dep.3, f32[32,256]{1,0:T(8,128)} %cor.3, f32[32,256]{1,0:T(8,128)} %cor.3, f32[32,256]{1,0:T(8,128)} %area.3, ...), custom_call_target="tpu_custom_call" | custom-call | tf_op jit(solution)/shard_map/pallas_call | solution.py:106
  2.2 1.9 %collective-permute-start = (f32[8,8,256]{2,1,0:T(8,128)}, f32[8,8,256]{2,1,0:T(8,128)S(1)}, u32[]{:S(2)}, u32[]{:S(2)}) collective-permute-start(f32[8,8,256]{2,1,0:T(8,128)} %get-tuple-element.7.near_in), channel_id=1, source_target_pairs={{0,8},{8,0},{16,24},{24,16},{32,40},{40,32},{48,56},{56,48},{64,72... | collective-permute-start | bytes 196616 | tf_op jit(solution)/shard_map/ppermute | solution.py:227
  4.1 19.6 %collective-permute-start.1 = (f32[8,8,256]{2,1,0:T(8,128)}, f32[8,8,256]{2,1,0:T(8,128)S(1)}, u32[]{:S(2)}, u32[]{:S(2)}) collective-permute-start(f32[8,8,256]{2,1,0:T(8,128)} %get-tuple-element.8.far_in), channel_id=1, source_target_pairs={{0,504},{8,16},{16,8},{24,32},{32,24},{40,48},{48,40},{56,64},{64,... | collective-permute-start | bytes 196616 | tf_op jit(solution)/shard_map/ppermute | solution.py:228
  23.7 2.6 %shard_map.96 = (f32[3,32,256]{2,1,0:T(8,128)}, bf16[4,2,32,128]{3,2,1,0:T(8,128)(2,1)}, f32[4,2,8,128]{3,2,1,0:T(8,128)}) custom-call(s32[1]{0:T(128)} %bitcast.odd_ref, f32[3,32,256]{2,1,0:T(8,128)} %ini.3, f32[32,256]{1,0:T(8,128)} %dep.3, f32[32,256]{1,0:T(8,128)} %cor.3, f32[32,256]{1,0:T(8,128)} %area.3, f32[2,32,256]{2,1,0:T(8,128)} %face.3, ...), custom_call_target="tpu_custom_call" | custom-call | tf_op jit(solution)/shard_map/pallas_call | solution.py:207
  26.3 2.2 %copy-done = bf16[64,2,128,128]{3,2,1,0:T(8,128)(2,1)S(1)} copy-done((bf16[64,2,128,128]{3,2,1,0:T(8,128)(2,1)S(1)}, bf16[64,2,128,128]{3,2,1,0:T(8,128)(2,1)}, u32[]{:S(2)}) %copy-start) | copy-done | bytes 4194328
  28.4 1.1 %fusion.27 = (bf16[8,2,128,128]{3,2,1,0:T(8,128)(2,1)}, bf16[8,2,128,128]{3,2,1,0:T(8,128)(2,1)}) fusion(bf16[64,2,128,128]{3,2,1,0:T(8,128)(2,1)S(1)} %copy-done), kind=kLoop, calls=%fused_computation.41 | loop fusion | bytes 2097152 | tf_op jit(solution)/shard_map/slice | solution.py:253
  30.2 1.2 %convert_add_fusion = f32[64,2]{0,1:T(2,128)} fusion(s32[64,2]{0,1:T(2,128)} %param.14), kind=kLoop, calls=%fused_computation.37 | loop fusion | flops 256 | bytes 1024 | tf_op jit(solution)/shard_map/add | solution.py:281
  31.5 0.8 copy.30
  32.2 0.7 reshape.72
  32.9 0.9 fusion.9
  33.9 0.5 fusion.15
  34.5 0.4 fusion.6
  34.9 0.6 copy-done.1
  35.5 0.6 copy-done.2
  36.2 2.5 %shard_map.97 = (f32[3,32,256]{2,1,0:T(8,128)}, bf16[4,2,32,128]{3,2,1,0:T(8,128)(2,1)}, f32[4,2,8,128]{3,2,1,0:T(8,128)}) custom-call(s32[1]{0:T(128)} %bitcast.odd_ref, f32[3,32,256]{2,1,0:T(8,128)} %ini.3, f32[32,256]{1,0:T(8,128)} %dep.3, f32[32,256]{1,0:T(8,128)} %cor.3, f32[32,256]{1,0:T(8,128)} %area.3, f32[2,32,256]{2,1,0:T(8,128)} %face.3, ...), custom_call_target="tpu_custom_call" | custom-call | tf_op jit(solution)/shard_map/pallas_call | solution.py:207
  38.7 0.8 convert_bitcast_fusion
  39.5 1.5 %fusion = f32[8,2,2,128,4]{3,4,2,1,0:T(4,128)S(1)} fusion(bf16[4,2,2,128,128]{4,3,2,1,0:T(8,128)(2,1)} %bitcast.35, bf16[4,2,2,128,128]{4,3,2,1,0:T(8,128)(2,1)} %bitcast.34, bf16[4,2,8,128,1]{3,2,1,0,4:T(8,128)(2,1)S(1)} %convert_bitcast_fusion), kind=kOutput, calls=%fused_computation.1 | convolution fusion | flops 4718592 | bytes 1130496 | tf_op jit(solution)/shard_map/shck,chrkt->chrst/dot_general | solution.py:246
  40.9 0.6 convolution_add_fusion
  41.6 0.2 reshape.69
  41.8 0.4 all_to_all.8
  42.2 48.0 %all_to_all.12 = f32[64,1,2176]{2,1,0:T(1,128)S(1)} all-to-all(f32[64,1,2176]{2,1,0:T(1,128)S(1)} %all_to_all.8), channel_id=1, replica_groups=mesh['tile'=64,'exp'=8] {'tile'}, dimensions={0} | all-to-all | bytes 1114112 | tf_op jit(solution)/shard_map/all_to_all | solution.py:287
  90.3 0.4 reshape_reshape.3
  90.8 0.3 fusion.4
  91.1 0.6 copy.32
  (27 shorter events, 1.0 us)
Async XLA Ops:
  2.2 32.7 %collective-permute-start = (f32[8,8,256]{2,1,0:T(8,128)}, f32[8,8,256]{2,1,0:T(8,128)S(1)}, u32[]{:S(2)}, u32[]{:S(2)}) collective-permute-start(f32[8,8,256]{2,1,0:T(8,128)} %get-tuple-element.7.near_in), channel_id=1, source_target_pairs={{0,8},{8,0},{16,24},{24,16},{32,40},{40,32},{48,56},{56,48},{64,72... | collective-permute-start | bytes 196616 | tf_op jit(solution)/shard_map/ppermute | solution.py:227
  4.1 30.8 %collective-permute-start.1 = (f32[8,8,256]{2,1,0:T(8,128)}, f32[8,8,256]{2,1,0:T(8,128)S(1)}, u32[]{:S(2)}, u32[]{:S(2)}) collective-permute-start(f32[8,8,256]{2,1,0:T(8,128)} %get-tuple-element.8.far_in), channel_id=1, source_target_pairs={{0,504},{8,16},{16,8},{24,32},{32,24},{40,48},{48,40},{56,64},{64,... | collective-permute-start | bytes 196616 | tf_op jit(solution)/shard_map/ppermute | solution.py:228
  26.2 2.2 %copy-start = (bf16[64,2,128,128]{3,2,1,0:T(8,128)(2,1)S(1)}, bf16[64,2,128,128]{3,2,1,0:T(8,128)(2,1)}, u32[]{:S(2)}) copy-start(bf16[64,2,128,128]{3,2,1,0:T(8,128)(2,1)} %param.15) | copy-start | bytes 12582916
  26.2 3.3 %copy-start.3 = (bf16[4,2,32,128]{3,2,1,0:T(8,128)(2,1)S(1)}, bf16[4,2,32,128]{3,2,1,0:T(8,128)(2,1)}, u32[]{:S(2)}) copy-start(bf16[4,2,32,128]{3,2,1,0:T(8,128)(2,1)} %get-tuple-element.9) | copy-start | bytes 196612
  26.2 3.3 %copy-start.4 = (s32[64,2]{0,1:T(2,128)S(1)}, s32[64,2]{0,1:T(2,128)}, u32[]{:S(2)}) copy-start(s32[64,2]{0,1:T(2,128)} %param.13) | copy-start | bytes 1540
  26.2 7.7 %slice-start = ((bf16[64,2,128,128]{3,2,1,0:T(8,128)(2,1)}), bf16[48,2,128,128]{3,2,1,0:T(8,128)(2,1)S(1)}, s32[]{:S(2)}) async-start(bf16[64,2,128,128]{3,2,1,0:T(8,128)(2,1)} %param.15), calls=%async_computation.1 | async-start | bytes 6291456 | tf_op jit(solution)/shard_map/slice | solution.py:252
  34.9 0.6 copy-start.1
  35.5 0.6 copy-start.2

commit v10 on v9

--- a/solution.py
+++ b/solution.py
@@ -190,10 +190,10 @@
                 HALO : HALO + own_rows, half * 128 : (half + 1) * 128
             ].astype(snap_ref.dtype)
             rounded = height[:, half * 128 : (half + 1) * 128].astype(snap_ref.dtype)
-            edge_ref[number, half, :STEPS] = rounded[HALO : HALO + STEPS].astype(jnp.float32)
-            edge_ref[number, half, STEPS:] = rounded[
-                HALO + own_rows - STEPS : HALO + own_rows
-            ].astype(jnp.float32)
+            wide = rounded.astype(jnp.float32)
+            for edge in range(2 * STEPS):
+                row = HALO + edge if edge < STEPS else HALO + own_rows - 2 * STEPS + edge
+                edge_ref[half, edge, pl.ds(number, 1), :] = wide[row : row + 1]
     final_ref[0] = height[HALO : HALO + own_rows]
     final_ref[1] = speed_x[HALO : HALO + own_rows]
     final_ref[2] = speed_y[HALO : HALO + own_rows]
@@ -203,7 +203,7 @@
     rows, lanes = depth_field.shape
     whole = lambda shape: pl.BlockSpec(shape, lambda: (0,) * len(shape))
     snap_shape = (STEPS, lanes // 128, rows, 128)
-    edge_shape = (STEPS, lanes // 128, 2 * STEPS, 128)
+    edge_shape = (lanes // 128, 2 * STEPS, 8, 128)
     return pl.pallas_call(
         stencil_kernel,
         out_shape=(
@@ -221,6 +221,29 @@
     )(odd, initial, depth_field, coriolis, cell_area, face_len, near_in, far_in)
 
 
+def edge_contrib_kernel(edge_ref, weight_ref, out_ref):
+    for block in range(weight_ref.shape[0]):
+        for half in range(weight_ref.shape[1]):
+            lhs = edge_ref[half, block].astype(jnp.bfloat16)
+            for part in range(weight_ref.shape[2]):
+                product = jnp.dot(
+                    lhs, weight_ref[block, half, part], preferred_element_type=jnp.float32
+                )
+                out_ref[block, half, part] = product[:STEPS]
+
+
+def edge_contrib(edge_snaps, edge_weights):
+    whole = lambda shape: pl.BlockSpec(shape, lambda: (0,) * len(shape))
+    blocks, halves, parts = edge_weights.shape[:3]
+    shape = (blocks, halves, parts, STEPS, 128)
+    return pl.pallas_call(
+        edge_contrib_kernel,
+        out_shape=jax.ShapeDtypeStruct(shape, jnp.float32),
+        in_specs=[whole(edge_snaps.shape), whole(edge_weights.shape)],
+        out_specs=whole(shape),
+    )(edge_snaps, edge_weights)
+
+
 def halo_exchange(near, far, axis):
     count = lax.axis_size(axis)
     odd = lax.axis_index(axis) % 2 == 1
@@ -269,7 +292,7 @@
     fields, _, edge_snaps = stencil(
         odd, initial, depth_field, coriolis, cell_area, face_len, near_in, far_in
     )
-    edge = contribute(edge_snaps.astype(jnp.bfloat16), edge_weights)
+    edge = edge_contrib(edge_snaps, edge_weights).reshape(-1, STEPS * 128)
     edge_pack = jnp.concatenate(
         [pack[:, : lo * per_column], pack[:, hi * per_column :]], axis=1
     )

time: 92.4 us -> 93.2 us (level)
  Pallas kernels: 6.65 us -> 8.93 us
  blocking collectives: 48 us -> 49.7 us
  matrix products: 4.22 us -> 2.95 us
  local copies, waits for them, and re-layouts: 8.06 us -> 7.1 us
  other arithmetic: 2.48 us -> 1.54 us
    pallas_call x0 -> x1, Pallas kernels: none -> 2.27 us  [edge_contrib(): pl.pallas_call(edge_contrib_kernel, out_shape=jax.ShapeDtypeStruct(shape,...]
    all_to_all x1, blocking collectives: 48 us -> 49.7 us  [on_device(): recv = lax.all_to_all(payload, 'tile', 0, 0, tiled=True)]
    dot_general x2 -> x1, matrix products: 1.97 us -> 0.52 us  [contribute(): jnp.einsum('shck,chrkt->chrst', snaps, grouped_part, preferred_element_ty...]
    add x1, other arithmetic: 1.25 us -> 0.01 us  [on_device(): offsets.reshape(-1, 1).astype(jnp.float32) + 1.0]
    add x2, local copies, waits for them, and re-layouts: 1.42 us -> 0.23 us  [on_device(): offsets.reshape(-1, 1).astype(jnp.float32) + 1.0]
    concatenate x0 -> x1, other arithmetic: none -> 1.07 us  [on_device(): edge_weights = jnp.concatenate([grouped[:lo], grouped[hi:]], axis=0)]
    unnamed x13 -> x19, local copies, waits for them, and re-layouts: 4.17 us -> 4.4 us
  transfers between devices with their start and end apart: 2 -> 2, of which waited for: 0 -> 0; matrix products, arithmetic and copies ran while one was open for 7% -> 5% of each run, Pallas kernels for 3% -> 3%
where the time goes in v10:
time: 93.2 us; the launch traced here: 92.6 us
  blocking collectives  49.7 us (53%)
  starting transfers between devices  21.5 us (23%)
  Pallas kernels  8.93 us (10%)
  local copies, waits for them, and re-layouts  7.1 us (8%)
  matrix products  2.95 us (3%)
  other arithmetic  1.54 us (2%)
    all_to_all x1, blocking collectives, on_device(): recv = lax.all_to_all(payload, 'tile', 0, 0, tiled=True)  49.7 us
    ppermute x1, starting transfers between devices, halo_exchange(): lax.ppermute(far, axis, [(i, (i + 1) % count if i % 2 else (i - 1) % coun...  19.6 us
    pallas_call x2, Pallas kernels, stencil(): pl.pallas_call(stencil_kernel, out_shape=(jax.ShapeDtypeStruct((3, rows,...  5.13 us
    unnamed x19, local copies, waits for them, and re-layouts  4.4 us
    pallas_call x1, Pallas kernels, edge_contrib(): pl.pallas_call(edge_contrib_kernel, out_shape=jax.ShapeDtypeStruct(shape,...  2.27 us
    ppermute x1, starting transfers between devices, halo_exchange(): near_in = lax.ppermute(near, axis, [(i, i ^ 1) for i in range(count)])  1.91 us
  transfers between devices with their start and end apart: 2, of which 0 were waited for; matrix products, arithmetic and copies ran while one was open for 5% of the time, Pallas kernels for 3%

profile of v10, /device:TPU:32, one launch (start us, length us, event | category | flops | bytes accessed | tf_op | source)
XLA Modules:
  0.0 92.6 jit_solution(1065312003962948537)
XLA Ops:
  0.6 1.5 %shard_map.95 = (f32[8,8,256]{2,1,0:T(8,128)}, f32[8,8,256]{2,1,0:T(8,128)}) custom-call(s32[1]{0:T(128)} %bitcast.odd_ref, f32[3,32,256]{2,1,0:T(8,128)} %ini.3, f32[3,32,256]{2,1,0:T(8,128)} %ini.3, f32[32,256]{1,0:T(8,128)} %dep.3, f32[32,256]{1,0:T(8,128)} %dep.3, f32[32,256]{1,0:T(8,128)} %cor.3, f32[32,256]{1,0:T(8,128)} %cor.3, f32[32,256]{1,0:T(8,128)} %area.3, ...), custom_call_target="tpu_custom_call" | custom-call | tf_op jit(solution)/shard_map/pallas_call | solution.py:106
  2.2 1.9 %collective-permute-start = (f32[8,8,256]{2,1,0:T(8,128)}, f32[8,8,256]{2,1,0:T(8,128)S(1)}, u32[]{:S(2)}, u32[]{:S(2)}) collective-permute-start(f32[8,8,256]{2,1,0:T(8,128)} %get-tuple-element.7.near_in), channel_id=1, source_target_pairs={{0,8},{8,0},{16,24},{24,16},{32,40},{40,32},{48,56},{56,48},{64,72... | collective-permute-start | bytes 196616 | tf_op jit(solution)/shard_map/ppermute | solution.py:250
  4.1 19.6 %collective-permute-start.1 = (f32[8,8,256]{2,1,0:T(8,128)}, f32[8,8,256]{2,1,0:T(8,128)S(1)}, u32[]{:S(2)}, u32[]{:S(2)}) collective-permute-start(f32[8,8,256]{2,1,0:T(8,128)} %get-tuple-element.8.far_in), channel_id=1, source_target_pairs={{0,504},{8,16},{16,8},{24,32},{32,24},{40,48},{48,40},{56,64},{64,... | collective-permute-start | bytes 196616 | tf_op jit(solution)/shard_map/ppermute | solution.py:251
  23.7 2.6 %shard_map.96 = (f32[3,32,256]{2,1,0:T(8,128)}, bf16[4,2,32,128]{3,2,1,0:T(8,128)(2,1)}, f32[2,8,8,128]{3,2,1,0:T(8,128)}) custom-call(s32[1]{0:T(128)} %bitcast.odd_ref, f32[3,32,256]{2,1,0:T(8,128)} %ini.3, f32[32,256]{1,0:T(8,128)} %dep.3, f32[32,256]{1,0:T(8,128)} %cor.3, f32[32,256]{1,0:T(8,128)} %area.3, f32[2,32,256]{2,1,0:T(8,128)} %face.3, ...), custom_call_target="tpu_custom_call" | custom-call | tf_op jit(solution)/shard_map/pallas_call | solution.py:207
  26.3 2.2 %copy-done = bf16[64,2,128,128]{3,2,1,0:T(8,128)(2,1)S(1)} copy-done((bf16[64,2,128,128]{3,2,1,0:T(8,128)(2,1)S(1)}, bf16[64,2,128,128]{3,2,1,0:T(8,128)(2,1)}, u32[]{:S(2)}) %copy-start) | copy-done | bytes 4194328
  28.4 1.1 %fusion.21 = (bf16[8,2,128,128]{3,2,1,0:T(8,128)(2,1)}, bf16[8,2,128,128]{3,2,1,0:T(8,128)(2,1)}) fusion(bf16[64,2,128,128]{3,2,1,0:T(8,128)(2,1)S(1)} %copy-done), kind=kLoop, calls=%fused_computation.35 | loop fusion | bytes 2097152 | tf_op jit(solution)/shard_map/slice | solution.py:276
  29.7 0.1 reshape.65
  29.8 0.2 convert_reduce_fusion
  30.5 0.3 fusion.5
  30.9 0.5 fusion.11
  31.4 0.4 fusion.2
  31.9 0.2 copy-done.2
  32.1 1.1 %pad_maximum_fusion.weight_ref = bf16[8,2,2,128,128]{4,3,2,1,0:T(8,128)(2,1)} fusion(bf16[4,2,2,128,128]{4,3,2,1,0:T(8,128)(2,1)S(1)} %bitcast.31, bf16[4,2,2,128,128]{4,3,2,1,0:T(8,128)(2,1)S(1)} %bitcast.30), kind=kLoop, calls=%fused_computation.1 | loop fusion | flops 524288 | bytes 2097152 | tf_op jit(solution)/shard_map/concatenate | solution.py:276
  33.2 0.6 copy-done.3
  33.8 0.6 copy-done.4
  34.4 2.6 %shard_map.97 = (f32[3,32,256]{2,1,0:T(8,128)}, bf16[4,2,32,128]{3,2,1,0:T(8,128)(2,1)}, f32[2,8,8,128]{3,2,1,0:T(8,128)}) custom-call(s32[1]{0:T(128)} %bitcast.odd_ref, f32[3,32,256]{2,1,0:T(8,128)} %ini.3, f32[32,256]{1,0:T(8,128)} %dep.3, f32[32,256]{1,0:T(8,128)} %cor.3, f32[32,256]{1,0:T(8,128)} %area.3, f32[2,32,256]{2,1,0:T(8,128)} %face.3, ...), custom_call_target="tpu_custom_call" | custom-call | tf_op jit(solution)/shard_map/pallas_call | solution.py:207
  37.0 2.3 %shard_map.98 = f32[8,2,2,4,128]{4,3,2,1,0:T(4,128)} custom-call(f32[2,8,8,128]{3,2,1,0:T(8,128)} %get-tuple-element.10.edge_ref, bf16[8,2,2,128,128]{4,3,2,1,0:T(8,128)(2,1)} %pad_maximum_fusion.weight_ref), custom_call_target="tpu_custom_call" | custom-call | tf_op jit(solution)/shard_map/pallas_call | solution.py:239
  39.2 1.5 %convolution_add_fusion = f32[256,512]{1,0:T(8,128)S(1)} fusion(f32[256,512]{1,0:T(8,128)S(1)} %fusion.2, f32[4,8,4,128]{3,2,1,0:T(4,128)} %bitcast.33, f32[256,16]{0,1:T(8,128)S(1)} %get-tuple-element.23, f32[256,16]{0,1:T(8,128)S(1)} %get-tuple-element.22), kind=kOutput, calls=%fused_computation | convolution fusion | flops 50470912 | bytes 1146880 | tf_op jit(solution)/shard_map/dot_general | solution.py:299
  40.7 0.2 reshape.69
  41.0 0.4 all_to_all.8
  41.4 49.7 %all_to_all.12 = f32[64,1,2176]{2,1,0:T(1,128)S(1)} all-to-all(f32[64,1,2176]{2,1,0:T(1,128)S(1)} %all_to_all.8), channel_id=1, replica_groups=mesh['tile'=64,'exp'=8] {'tile'}, dimensions={0} | all-to-all | bytes 1114112 | tf_op jit(solution)/shard_map/all_to_all | solution.py:310
  91.2 0.4 reshape_reshape.3
  91.7 0.3 fusion
  92.0 0.6 copy.28
  (33 shorter events, 1.0 us)
Async XLA Ops:
  2.2 31.0 %collective-permute-start = (f32[8,8,256]{2,1,0:T(8,128)}, f32[8,8,256]{2,1,0:T(8,128)S(1)}, u32[]{:S(2)}, u32[]{:S(2)}) collective-permute-start(f32[8,8,256]{2,1,0:T(8,128)} %get-tuple-element.7.near_in), channel_id=1, source_target_pairs={{0,8},{8,0},{16,24},{24,16},{32,40},{40,32},{48,56},{56,48},{64,72... | collective-permute-start | bytes 196616 | tf_op jit(solution)/shard_map/ppermute | solution.py:250
  4.1 29.1 %collective-permute-start.1 = (f32[8,8,256]{2,1,0:T(8,128)}, f32[8,8,256]{2,1,0:T(8,128)S(1)}, u32[]{:S(2)}, u32[]{:S(2)}) collective-permute-start(f32[8,8,256]{2,1,0:T(8,128)} %get-tuple-element.8.far_in), channel_id=1, source_target_pairs={{0,504},{8,16},{16,8},{24,32},{32,24},{40,48},{48,40},{56,64},{64,... | collective-permute-start | bytes 196616 | tf_op jit(solution)/shard_map/ppermute | solution.py:251
  26.2 2.2 %copy-start = (bf16[64,2,128,128]{3,2,1,0:T(8,128)(2,1)S(1)}, bf16[64,2,128,128]{3,2,1,0:T(8,128)(2,1)}, u32[]{:S(2)}) copy-start(bf16[64,2,128,128]{3,2,1,0:T(8,128)(2,1)} %param.15) | copy-start | bytes 12582916
  26.2 3.3 %copy-start.5 = (bf16[4,2,32,128]{3,2,1,0:T(8,128)(2,1)S(1)}, bf16[4,2,32,128]{3,2,1,0:T(8,128)(2,1)}, u32[]{:S(2)}) copy-start(bf16[4,2,32,128]{3,2,1,0:T(8,128)(2,1)} %get-tuple-element.9) | copy-start | bytes 196612
  26.2 3.3 %copy-start.6 = (s32[64,2]{0,1:T(2,128)S(1)}, s32[64,2]{0,1:T(2,128)}, u32[]{:S(2)}) copy-start(s32[64,2]{0,1:T(2,128)} %param.13) | copy-start | bytes 1540
  26.2 4.0 %copy-start.7 = (s32[64,2]{0,1:T(2,128)S(1)}, s32[64,2]{0,1:T(2,128)}, u32[]{:S(2)}) copy-start(s32[64,2]{0,1:T(2,128)} %param.14) | copy-start | bytes 1540
  26.3 4.7 %slice-start = ((bf16[64,2,128,128]{3,2,1,0:T(8,128)(2,1)}), bf16[48,2,128,128]{3,2,1,0:T(8,128)(2,1)S(1)}, s32[]{:S(2)}) async-start(bf16[64,2,128,128]{3,2,1,0:T(8,128)(2,1)} %param.15), calls=%async_computation.1 | async-start | bytes 6291456 | tf_op jit(solution)/shard_map/slice | solution.py:275
  30.9 1.1 %copy-start.1 = (bf16[8,2,128,128]{3,2,1,0:T(8,128)(2,1)S(1)}, bf16[8,2,128,128]{3,2,1,0:T(8,128)(2,1)}, u32[]{:S(2)}) copy-start(bf16[8,2,128,128]{3,2,1,0:T(8,128)(2,1)} %get-tuple-element.20) | copy-start | bytes 1572868
  30.9 1.2 %copy-start.2 = (bf16[8,2,128,128]{3,2,1,0:T(8,128)(2,1)S(1)}, bf16[8,2,128,128]{3,2,1,0:T(8,128)(2,1)}, u32[]{:S(2)}) copy-start(bf16[8,2,128,128]{3,2,1,0:T(8,128)(2,1)} %get-tuple-element.21) | copy-start | bytes 1572868
  33.2 0.6 copy-start.3
  33.8 0.6 copy-start.4

commit v11 on v9

--- a/solution.py
+++ b/solution.py
@@ -199,25 +199,37 @@
     final_ref[2] = speed_y[HALO : HALO + own_rows]
 
 
-def stencil(odd, initial, depth_field, coriolis, cell_area, face_len, near_in, far_in):
+def stencil(odd, initial, depth_field, coriolis, cell_area, face_len, near_in, far_in, inner):
     rows, lanes = depth_field.shape
     whole = lambda shape: pl.BlockSpec(shape, lambda: (0,) * len(shape))
-    snap_shape = (STEPS, lanes // 128, rows, 128)
-    edge_shape = (STEPS, lanes // 128, 2 * STEPS, 128)
+    shapes = [
+        ((3, rows, lanes), jnp.float32),
+        ((STEPS, lanes // 128, rows, 128), jnp.bfloat16),
+        ((STEPS, lanes // 128, 2 * STEPS, 128), jnp.float32),
+    ]
+    kept = [1] if inner else [0, 2]
+    dropped = [i for i in range(3) if i not in kept]
+
+    def kernel(*refs):
+        ins, outs, rest = refs[:8], refs[8 : 8 + len(kept)], refs[8 + len(kept) :]
+        slots = [None] * 3
+        for i, ref in zip(kept, outs):
+            slots[i] = ref
+        for i, ref in zip(dropped, rest[1:]):
+            slots[i] = ref
+        stencil_kernel(*ins, *slots, rest[0])
+
     return pl.pallas_call(
-        stencil_kernel,
-        out_shape=(
-            jax.ShapeDtypeStruct((3, rows, lanes), jnp.float32),
-            jax.ShapeDtypeStruct(snap_shape, jnp.bfloat16),
-            jax.ShapeDtypeStruct(edge_shape, jnp.float32),
-        ),
+        kernel,
+        out_shape=tuple(jax.ShapeDtypeStruct(*shapes[i]) for i in kept),
         in_specs=[
             pl.BlockSpec(memory_space=pltpu.SMEM),
             whole(initial.shape), whole(depth_field.shape), whole(coriolis.shape),
             whole(cell_area.shape), whole(face_len.shape), whole(near_in.shape), whole(far_in.shape),
         ],
-        out_specs=(whole((3, rows, lanes)), whole(snap_shape), whole(edge_shape)),
-        scratch_shapes=[pltpu.VMEM((CHANNELS, rows + 2 * HALO, lanes), jnp.float32)],
+        out_specs=tuple(whole(shapes[i][0]) for i in kept),
+        scratch_shapes=[pltpu.VMEM((CHANNELS, rows + 2 * HALO, lanes), jnp.float32)]
+        + [pltpu.VMEM(*shapes[i]) for i in dropped],
     )(odd, initial, depth_field, coriolis, cell_area, face_len, near_in, far_in)
 
 
@@ -248,7 +260,9 @@
         )
         return part.reshape(-1, STEPS * 128)
 
-    _, inner_snaps, _ = stencil(odd, initial, depth_field, coriolis, cell_area, face_len, near, far)
+    (inner_snaps,) = stencil(
+        odd, initial, depth_field, coriolis, cell_area, face_len, near, far, True
+    )
     inner = contribute(inner_snaps[:, :, lo:hi], grouped[lo:hi])
     edge_weights = jnp.concatenate([grouped[:lo], grouped[hi:]], axis=0)
     n_tile = lax.axis_size("tile")
@@ -266,8 +280,8 @@
         precision=lax.Precision.HIGHEST,
         preferred_element_type=jnp.float32,
     )
-    fields, _, edge_snaps = stencil(
-        odd, initial, depth_field, coriolis, cell_area, face_len, near_in, far_in
+    fields, edge_snaps = stencil(
+        odd, initial, depth_field, coriolis, cell_area, face_len, near_in, far_in, False
     )
     edge = contribute(edge_snaps.astype(jnp.bfloat16), edge_weights)
     edge_pack = jnp.concatenate(

time: 92.4 us -> 92.4 us (level)
  no operation moved by 1% of the time
where the time goes in v11:
time: 92.4 us; the launch traced here: 91.7 us
  blocking collectives  48.1 us (52%)
  starting transfers between devices  21.5 us (23%)
  local copies, waits for them, and re-layouts  8.03 us (9%)
  Pallas kernels  6.48 us (7%)
  matrix products  4.23 us (5%)
  other arithmetic  2.48 us (3%)
    all_to_all x1, blocking collectives, on_device(): recv = lax.all_to_all(payload, 'tile', 0, 0, tiled=True)  48.1 us
    ppermute x1, starting transfers between devices, halo_exchange(): lax.ppermute(far, axis, [(i, (i + 1) % count if i % 2 else (i - 1) % coun...  19.6 us
    pallas_call x2, Pallas kernels, stencil(): pl.pallas_call(kernel, out_shape=tuple((jax.ShapeDtypeStruct(*shapes[i])...  4.95 us
    unnamed x13, local copies, waits for them, and re-layouts  4.15 us
    dot_general x2, matrix products, contribute(): jnp.einsum('shck,chrkt->chrst', snaps, grouped_part, preferred_element_ty...  1.97 us
    ppermute x1, starting transfers between devices, halo_exchange(): near_in = lax.ppermute(near, axis, [(i, i ^ 1) for i in range(count)])  1.91 us
  transfers between devices with their start and end apart: 2, of which 0 were waited for; matrix products, arithmetic and copies ran while one was open for 7% of the time, Pallas kernels for 3%

profile of v11, /device:TPU:32, one launch (start us, length us, event | category | flops | bytes accessed | tf_op | source)
XLA Modules:
  0.0 91.7 jit_solution(3091129319595831694)
XLA Ops:
  0.6 1.5 %shard_map.95 = (f32[8,8,256]{2,1,0:T(8,128)}, f32[8,8,256]{2,1,0:T(8,128)}) custom-call(s32[1]{0:T(128)} %bitcast.odd_ref.refs_0_, f32[3,32,256]{2,1,0:T(8,128)} %refs_1_.3, f32[3,32,256]{2,1,0:T(8,128)} %refs_1_.3, f32[32,256]{1,0:T(8,128)} %refs_2_.3, f32[32,256]{1,0:T(8,128)} %refs_2_.3, f32[32,256]{1,0:T(8,128)} %refs_3_.3, f32[32,256]{1,0:T(8,128)} %refs_3_.3, ...), custom_call_target="tpu_custom_call" | custom-call | tf_op jit(solution)/shard_map/pallas_call | solution.py:106
  2.2 1.9 %collective-permute-start = (f32[8,8,256]{2,1,0:T(8,128)}, f32[8,8,256]{2,1,0:T(8,128)S(1)}, u32[]{:S(2)}, u32[]{:S(2)}) collective-permute-start(f32[8,8,256]{2,1,0:T(8,128)} %get-tuple-element.6.refs_6_), channel_id=1, source_target_pairs={{0,8},{8,0},{16,24},{24,16},{32,40},{40,32},{48,56},{56,48},{64,72... | collective-permute-start | bytes 196616 | tf_op jit(solution)/shard_map/ppermute | solution.py:239
  4.1 19.6 %collective-permute-start.1 = (f32[8,8,256]{2,1,0:T(8,128)}, f32[8,8,256]{2,1,0:T(8,128)S(1)}, u32[]{:S(2)}, u32[]{:S(2)}) collective-permute-start(f32[8,8,256]{2,1,0:T(8,128)} %get-tuple-element.7.refs_7_), channel_id=1, source_target_pairs={{0,504},{8,16},{16,8},{24,32},{32,24},{40,48},{48,40},{56,64},{64,... | collective-permute-start | bytes 196616 | tf_op jit(solution)/shard_map/ppermute | solution.py:240
  23.7 2.4 %shard_map.96 = bf16[4,2,32,128]{3,2,1,0:T(8,128)(2,1)} custom-call(s32[1]{0:T(128)} %bitcast.odd_ref.refs_0_, f32[3,32,256]{2,1,0:T(8,128)} %refs_1_.3, f32[32,256]{1,0:T(8,128)} %refs_2_.3, f32[32,256]{1,0:T(8,128)} %refs_3_.3, f32[32,256]{1,0:T(8,128)} %refs_4_.3, f32[2,32,256]{2,1,0:T(8,128)} %refs_5_.3, f32[8,8,256]{2,1,0:T(8,128)} %get-tuple-element.6.refs_6_, ...), custom_call_target="tpu_custom_call" | custom-call | tf_op jit(solution)/shard_map/pallas_call | solution.py:222
  26.1 2.2 %copy-done = bf16[64,2,128,128]{3,2,1,0:T(8,128)(2,1)S(1)} copy-done((bf16[64,2,128,128]{3,2,1,0:T(8,128)(2,1)S(1)}, bf16[64,2,128,128]{3,2,1,0:T(8,128)(2,1)}, u32[]{:S(2)}) %copy-start) | copy-done | bytes 4194328
  28.3 1.1 %fusion.27 = (bf16[8,2,128,128]{3,2,1,0:T(8,128)(2,1)}, bf16[8,2,128,128]{3,2,1,0:T(8,128)(2,1)}) fusion(bf16[64,2,128,128]{3,2,1,0:T(8,128)(2,1)S(1)} %copy-done), kind=kLoop, calls=%fused_computation.41 | loop fusion | bytes 2097152 | tf_op jit(solution)/shard_map/slice | solution.py:267
  30.1 1.2 %convert_add_fusion = f32[64,2]{0,1:T(2,128)} fusion(s32[64,2]{0,1:T(2,128)} %param.14), kind=kLoop, calls=%fused_computation.37 | loop fusion | flops 256 | bytes 1024 | tf_op jit(solution)/shard_map/add | solution.py:295
  31.3 0.8 copy.30
  32.1 0.7 reshape.72
  32.7 0.9 fusion.9
  33.8 0.5 fusion.15
  34.3 0.4 fusion.6
  34.8 0.6 copy-done.2
  35.4 0.6 copy-done.3
  36.0 2.5 %shard_map.97 = (f32[3,32,256]{2,1,0:T(8,128)}, f32[4,2,8,128]{3,2,1,0:T(8,128)}) custom-call(s32[1]{0:T(128)} %bitcast.odd_ref.refs_0_, f32[3,32,256]{2,1,0:T(8,128)} %refs_1_.3, f32[32,256]{1,0:T(8,128)} %refs_2_.3, f32[32,256]{1,0:T(8,128)} %refs_3_.3, f32[32,256]{1,0:T(8,128)} %refs_4_.3, f32[2,32,256]{2,1,0:T(8,128)} %refs_5_.3, ...), custom_call_target="tpu_custom_call" | custom-call | tf_op jit(solution)/shard_map/pallas_call | solution.py:222
  38.5 0.8 convert_bitcast_fusion
  39.3 1.5 %fusion = f32[8,2,2,128,4]{3,4,2,1,0:T(4,128)S(1)} fusion(bf16[4,2,2,128,128]{4,3,2,1,0:T(8,128)(2,1)} %bitcast.35, bf16[4,2,2,128,128]{4,3,2,1,0:T(8,128)(2,1)} %bitcast.34, bf16[4,2,8,128,1]{3,2,1,0,4:T(8,128)(2,1)S(1)} %convert_bitcast_fusion), kind=kOutput, calls=%fused_computation.1 | convolution fusion | flops 4718592 | bytes 1130496 | tf_op jit(solution)/shard_map/shck,chrkt->chrst/dot_general | solution.py:258
  40.7 0.6 convolution_add_fusion
  41.4 0.2 reshape.69
  41.7 0.4 all_to_all.8
  42.1 48.1 %all_to_all.12 = f32[64,1,2176]{2,1,0:T(1,128)S(1)} all-to-all(f32[64,1,2176]{2,1,0:T(1,128)S(1)} %all_to_all.8), channel_id=1, replica_groups=mesh['tile'=64,'exp'=8] {'tile'}, dimensions={0} | all-to-all | bytes 1114112 | tf_op jit(solution)/shard_map/all_to_all | solution.py:301
  90.3 0.4 reshape_reshape.3
  90.7 0.3 fusion.4
  91.0 0.6 copy.32
  (27 shorter events, 1.0 us)
Async XLA Ops:
  2.2 32.6 %collective-permute-start = (f32[8,8,256]{2,1,0:T(8,128)}, f32[8,8,256]{2,1,0:T(8,128)S(1)}, u32[]{:S(2)}, u32[]{:S(2)}) collective-permute-start(f32[8,8,256]{2,1,0:T(8,128)} %get-tuple-element.6.refs_6_), channel_id=1, source_target_pairs={{0,8},{8,0},{16,24},{24,16},{32,40},{40,32},{48,56},{56,48},{64,72... | collective-permute-start | bytes 196616 | tf_op jit(solution)/shard_map/ppermute | solution.py:239
  4.1 30.7 %collective-permute-start.1 = (f32[8,8,256]{2,1,0:T(8,128)}, f32[8,8,256]{2,1,0:T(8,128)S(1)}, u32[]{:S(2)}, u32[]{:S(2)}) collective-permute-start(f32[8,8,256]{2,1,0:T(8,128)} %get-tuple-element.7.refs_7_), channel_id=1, source_target_pairs={{0,504},{8,16},{16,8},{24,32},{32,24},{40,48},{48,40},{56,64},{64,... | collective-permute-start | bytes 196616 | tf_op jit(solution)/shard_map/ppermute | solution.py:240
  26.1 2.2 %copy-start = (bf16[64,2,128,128]{3,2,1,0:T(8,128)(2,1)S(1)}, bf16[64,2,128,128]{3,2,1,0:T(8,128)(2,1)}, u32[]{:S(2)}) copy-start(bf16[64,2,128,128]{3,2,1,0:T(8,128)(2,1)} %param.15) | copy-start | bytes 12582916
  26.1 3.3 %copy-start.1 = (bf16[4,2,32,128]{3,2,1,0:T(8,128)(2,1)S(1)}, bf16[4,2,32,128]{3,2,1,0:T(8,128)(2,1)}, u32[]{:S(2)}) copy-start(bf16[4,2,32,128]{3,2,1,0:T(8,128)(2,1)} %shard_map.96) | copy-start | bytes 196612
  26.1 3.3 %copy-start.4 = (s32[64,2]{0,1:T(2,128)S(1)}, s32[64,2]{0,1:T(2,128)}, u32[]{:S(2)}) copy-start(s32[64,2]{0,1:T(2,128)} %param.13) | copy-start | bytes 1540
  26.1 7.7 %slice-start = ((bf16[64,2,128,128]{3,2,1,0:T(8,128)(2,1)}), bf16[48,2,128,128]{3,2,1,0:T(8,128)(2,1)S(1)}, s32[]{:S(2)}) async-start(bf16[64,2,128,128]{3,2,1,0:T(8,128)(2,1)} %param.15), calls=%async_computation.1 | async-start | bytes 6291456 | tf_op jit(solution)/shard_map/slice | solution.py:266
  34.8 0.6 copy-start.2
  35.4 0.6 copy-start.3

commit v12 on v8

--- a/solution.py
+++ b/solution.py
@@ -192,23 +192,30 @@
     final_ref[2] = speed_y[HALO : HALO + own_rows]
 
 
-def stencil(odd, initial, depth_field, coriolis, cell_area, face_len, near_in, far_in):
+def stencil(odd, initial, depth_field, coriolis, cell_area, face_len, near_in, far_in, inner):
     rows, lanes = depth_field.shape
     whole = lambda shape: pl.BlockSpec(shape, lambda: (0,) * len(shape))
-    snap_shape = (STEPS, lanes // 128, rows, 128)
+    final_shape = ((3, rows, lanes), jnp.float32)
+    snap_shape = ((STEPS, lanes // 128, rows, 128), jnp.bfloat16)
+    kept = [snap_shape] if inner else [final_shape, snap_shape]
+
+    def kernel(*refs):
+        if inner:
+            stencil_kernel(*refs[:8], refs[10], refs[8], refs[9])
+        else:
+            stencil_kernel(*refs)
+
     return pl.pallas_call(
-        stencil_kernel,
-        out_shape=(
-            jax.ShapeDtypeStruct((3, rows, lanes), jnp.float32),
-            jax.ShapeDtypeStruct(snap_shape, jnp.bfloat16),
-        ),
+        kernel,
+        out_shape=tuple(jax.ShapeDtypeStruct(*k) for k in kept),
         in_specs=[
             pl.BlockSpec(memory_space=pltpu.SMEM),
             whole(initial.shape), whole(depth_field.shape), whole(coriolis.shape),
             whole(cell_area.shape), whole(face_len.shape), whole(near_in.shape), whole(far_in.shape),
         ],
-        out_specs=(whole((3, rows, lanes)), whole(snap_shape)),
-        scratch_shapes=[pltpu.VMEM((CHANNELS, rows + 2 * HALO, lanes), jnp.float32)],
+        out_specs=tuple(whole(k[0]) for k in kept),
+        scratch_shapes=[pltpu.VMEM((CHANNELS, rows + 2 * HALO, lanes), jnp.float32)]
+        + ([pltpu.VMEM(*final_shape)] if inner else []),
     )(odd, initial, depth_field, coriolis, cell_area, face_len, near_in, far_in)
 
 
@@ -239,7 +246,9 @@
         )
         return part.reshape(-1, STEPS * 128)
 
-    _, inner_snaps = stencil(odd, initial, depth_field, coriolis, cell_area, face_len, near, far)
+    (inner_snaps,) = stencil(
+        odd, initial, depth_field, coriolis, cell_area, face_len, near, far, True
+    )
     inner = contribute(inner_snaps[:, :, lo:hi], grouped[lo:hi])
     edge_weights = jnp.concatenate([grouped[:lo], grouped[hi:]], axis=0)
     n_tile = lax.axis_size("tile")
@@ -257,7 +266,9 @@
         precision=lax.Precision.HIGHEST,
         preferred_element_type=jnp.float32,
     )
-    fields, snaps = stencil(odd, initial, depth_field, coriolis, cell_area, face_len, near_in, far_in)
+    fields, snaps = stencil(
+        odd, initial, depth_field, coriolis, cell_area, face_len, near_in, far_in, False
+    )
     edge = contribute(
         jnp.concatenate([snaps[:, :, :lo], snaps[:, :, hi:]], axis=2), edge_weights
     )

time: 92.3 us -> 92.4 us (level)
  no operation moved by 1% of the time
where the time goes in v12:
time: 92.4 us; the launch traced here: 91.7 us
  blocking collectives  48.2 us (52%)
  starting transfers between devices  21.5 us (23%)
  local copies, waits for them, and re-layouts  8.8 us (10%)
  Pallas kernels  6.37 us (7%)
  matrix products  4.23 us (5%)
  other arithmetic  1.73 us (2%)
    all_to_all x1, blocking collectives, on_device(): recv = lax.all_to_all(payload, 'tile', 0, 0, tiled=True)  48.2 us
    ppermute x1, starting transfers between devices, halo_exchange(): lax.ppermute(far, axis, [(i, (i + 1) % count if i % 2 else (i - 1) % coun...  19.6 us
    pallas_call x2, Pallas kernels, stencil(): pl.pallas_call(kernel, out_shape=tuple((jax.ShapeDtypeStruct(*k) for k in...  4.83 us
    unnamed x13, local copies, waits for them, and re-layouts  4.17 us
    dot_general x2, matrix products, contribute(): jnp.einsum('shck,chrkt->chrst', snaps, grouped_part, preferred_element_ty...  1.97 us
    ppermute x1, starting transfers between devices, halo_exchange(): near_in = lax.ppermute(near, axis, [(i, i ^ 1) for i in range(count)])  1.91 us
  transfers between devices with their start and end apart: 2, of which 0 were waited for; matrix products, arithmetic and copies ran while one was open for 7% of the time, Pallas kernels for 3%

profile of v12, /device:TPU:32, one launch (start us, length us, event | category | flops | bytes accessed | tf_op | source)
XLA Modules:
  0.0 91.7 jit_solution(1831605673473106043)
XLA Ops:
  0.6 1.5 %shard_map.95 = (f32[8,8,256]{2,1,0:T(8,128)}, f32[8,8,256]{2,1,0:T(8,128)}) custom-call(s32[1]{0:T(128)} %bitcast.odd_ref.refs_0_, f32[3,32,256]{2,1,0:T(8,128)} %refs_1_.3, f32[3,32,256]{2,1,0:T(8,128)} %refs_1_.3, f32[32,256]{1,0:T(8,128)} %refs_2_.3, f32[32,256]{1,0:T(8,128)} %refs_2_.3, f32[32,256]{1,0:T(8,128)} %refs_3_.3, f32[32,256]{1,0:T(8,128)} %refs_3_.3, ...), custom_call_target="tpu_custom_call" | custom-call | tf_op jit(solution)/shard_map/pallas_call | solution.py:106
  2.2 1.9 %collective-permute-start = (f32[8,8,256]{2,1,0:T(8,128)}, f32[8,8,256]{2,1,0:T(8,128)S(1)}, u32[]{:S(2)}, u32[]{:S(2)}) collective-permute-start(f32[8,8,256]{2,1,0:T(8,128)} %get-tuple-element.6.refs_6_), channel_id=1, source_target_pairs={{0,8},{8,0},{16,24},{24,16},{32,40},{40,32},{48,56},{56,48},{64,72... | collective-permute-start | bytes 196616 | tf_op jit(solution)/shard_map/ppermute | solution.py:225
  4.1 19.6 %collective-permute-start.1 = (f32[8,8,256]{2,1,0:T(8,128)}, f32[8,8,256]{2,1,0:T(8,128)S(1)}, u32[]{:S(2)}, u32[]{:S(2)}) collective-permute-start(f32[8,8,256]{2,1,0:T(8,128)} %get-tuple-element.7.refs_7_), channel_id=1, source_target_pairs={{0,504},{8,16},{16,8},{24,32},{32,24},{40,48},{48,40},{56,64},{64,... | collective-permute-start | bytes 196616 | tf_op jit(solution)/shard_map/ppermute | solution.py:226
  23.7 2.3 %shard_map.96 = bf16[4,2,32,128]{3,2,1,0:T(8,128)(2,1)} custom-call(s32[1]{0:T(128)} %bitcast.odd_ref.refs_0_, f32[3,32,256]{2,1,0:T(8,128)} %refs_1_.3, f32[32,256]{1,0:T(8,128)} %refs_2_.3, f32[32,256]{1,0:T(8,128)} %refs_3_.3, f32[32,256]{1,0:T(8,128)} %refs_4_.3, f32[2,32,256]{2,1,0:T(8,128)} %refs_5_.3, f32[8,8,256]{2,1,0:T(8,128)} %get-tuple-element.6.refs_6_, ...), custom_call_target="tpu_custom_call" | custom-call | tf_op jit(solution)/shard_map/pallas_call | solution.py:208
  26.0 2.2 %copy-done = bf16[64,2,128,128]{3,2,1,0:T(8,128)(2,1)S(1)} copy-done((bf16[64,2,128,128]{3,2,1,0:T(8,128)(2,1)S(1)}, bf16[64,2,128,128]{3,2,1,0:T(8,128)(2,1)}, u32[]{:S(2)}) %copy-start) | copy-done | bytes 4194328
  28.2 1.1 %fusion.27 = (bf16[8,2,128,128]{3,2,1,0:T(8,128)(2,1)}, bf16[8,2,128,128]{3,2,1,0:T(8,128)(2,1)}) fusion(bf16[64,2,128,128]{3,2,1,0:T(8,128)(2,1)S(1)} %copy-done), kind=kLoop, calls=%fused_computation.41 | loop fusion | bytes 2097152 | tf_op jit(solution)/shard_map/slice | solution.py:253
  30.0 1.2 %convert_add_fusion = f32[64,2]{0,1:T(2,128)} fusion(s32[64,2]{0,1:T(2,128)} %param.14), kind=kLoop, calls=%fused_computation.37 | loop fusion | flops 256 | bytes 1024 | tf_op jit(solution)/shard_map/add | solution.py:283
  31.3 0.8 copy.30
  32.0 0.7 reshape.72
  32.7 0.9 fusion.9
  33.7 0.5 fusion.15
  34.2 0.4 fusion.6
  34.7 0.6 copy-done.2
  35.3 0.6 copy-done.3
  35.9 2.5 %shard_map.97 = (f32[3,32,256]{2,1,0:T(8,128)}, bf16[4,2,32,128]{3,2,1,0:T(8,128)(2,1)}) custom-call(s32[1]{0:T(128)} %bitcast.odd_ref.refs_0_, f32[3,32,256]{2,1,0:T(8,128)} %refs_1_.3, f32[32,256]{1,0:T(8,128)} %refs_2_.3, f32[32,256]{1,0:T(8,128)} %refs_3_.3, f32[32,256]{1,0:T(8,128)} %refs_4_.3, f32[2,32,256]{2,1,0:T(8,128)} %refs_5_.3, ...), custom_call_target="tpu_custom_call" | custom-call | tf_op jit(solution)/shard_map/pallas_call | solution.py:208
  38.4 0.7 fusion.29
  39.2 1.5 %fusion = f32[8,2,2,128,4]{3,4,2,1,0:T(4,128)S(1)} fusion(bf16[4,2,2,128,128]{4,3,2,1,0:T(8,128)(2,1)} %bitcast.35, bf16[4,2,2,128,128]{4,3,2,1,0:T(8,128)(2,1)} %bitcast.34, bf16[4,2,8,128,1]{3,2,1,0,4:T(8,128)(2,1)S(1)} %maximum_bitcast_fusion), kind=kOutput, calls=%fused_computation.1 | convolution fusion | flops 4718592 | bytes 1130496 | tf_op jit(solution)/shard_map/shck,chrkt->chrst/dot_general | solution.py:244
  40.7 0.6 convolution_add_fusion
  41.3 0.2 reshape.69
  41.6 0.4 all_to_all.8
  42.0 48.2 %all_to_all.12 = f32[64,1,2176]{2,1,0:T(1,128)S(1)} all-to-all(f32[64,1,2176]{2,1,0:T(1,128)S(1)} %all_to_all.8), channel_id=1, replica_groups=mesh['tile'=64,'exp'=8] {'tile'}, dimensions={0} | all-to-all | bytes 1114112 | tf_op jit(solution)/shard_map/all_to_all | solution.py:289
  90.3 0.4 reshape_reshape.3
  90.7 0.3 fusion.4
  91.0 0.6 copy.32
  (28 shorter events, 1.0 us)
Async XLA Ops:
  2.2 32.5 %collective-permute-start = (f32[8,8,256]{2,1,0:T(8,128)}, f32[8,8,256]{2,1,0:T(8,128)S(1)}, u32[]{:S(2)}, u32[]{:S(2)}) collective-permute-start(f32[8,8,256]{2,1,0:T(8,128)} %get-tuple-element.6.refs_6_), channel_id=1, source_target_pairs={{0,8},{8,0},{16,24},{24,16},{32,40},{40,32},{48,56},{56,48},{64,72... | collective-permute-start | bytes 196616 | tf_op jit(solution)/shard_map/ppermute | solution.py:225
  4.1 30.6 %collective-permute-start.1 = (f32[8,8,256]{2,1,0:T(8,128)}, f32[8,8,256]{2,1,0:T(8,128)S(1)}, u32[]{:S(2)}, u32[]{:S(2)}) collective-permute-start(f32[8,8,256]{2,1,0:T(8,128)} %get-tuple-element.7.refs_7_), channel_id=1, source_target_pairs={{0,504},{8,16},{16,8},{24,32},{32,24},{40,48},{48,40},{56,64},{64,... | collective-permute-start | bytes 196616 | tf_op jit(solution)/shard_map/ppermute | solution.py:226
  26.0 2.2 %copy-start = (bf16[64,2,128,128]{3,2,1,0:T(8,128)(2,1)S(1)}, bf16[64,2,128,128]{3,2,1,0:T(8,128)(2,1)}, u32[]{:S(2)}) copy-start(bf16[64,2,128,128]{3,2,1,0:T(8,128)(2,1)} %param.15) | copy-start | bytes 12582916
  26.0 3.3 %copy-start.1 = (bf16[4,2,32,128]{3,2,1,0:T(8,128)(2,1)S(1)}, bf16[4,2,32,128]{3,2,1,0:T(8,128)(2,1)}, u32[]{:S(2)}) copy-start(bf16[4,2,32,128]{3,2,1,0:T(8,128)(2,1)} %shard_map.96) | copy-start | bytes 196612
  26.0 3.3 %copy-start.4 = (s32[64,2]{0,1:T(2,128)S(1)}, s32[64,2]{0,1:T(2,128)}, u32[]{:S(2)}) copy-start(s32[64,2]{0,1:T(2,128)} %param.13) | copy-start | bytes 1540
  26.0 7.7 %slice-start = ((bf16[64,2,128,128]{3,2,1,0:T(8,128)(2,1)}), bf16[48,2,128,128]{3,2,1,0:T(8,128)(2,1)S(1)}, s32[]{:S(2)}) async-start(bf16[64,2,128,128]{3,2,1,0:T(8,128)(2,1)} %param.15), calls=%async_computation.1 | async-start | bytes 6291456 | tf_op jit(solution)/shard_map/slice | solution.py:252
  34.7 0.6 copy-start.2
  35.3 0.6 copy-start.3
